TPU v7x, 512 devices: a whole 4x8x8 slice. The times are simulated.
512 devices in a mesh: seq: 32 (over y_hi, z, core), chan: 16 (over x, y_lo).
Axes of the slice: x: 4, y: 8 (y_hi: 2, y_lo: 4; y = y_hi * 4 + y_lo), z: 8, core: 2. Of those that a mesh axis runs over, the one named last changes fastest.
Arguments:
- signal: bfloat16 [2048, 32768], P('chan', 'seq'), may hold values from -6 to 6
- spectrum: bfloat16 [2, 2048, 64, 1024], P(None, 'chan', 'seq'), may hold values from -5 to 5
- skip_gain: float32 [2048], P('chan'), may hold values from -4 to 4
Outputs:
- filtered: bfloat16 [2048, 32768], P('chan', 'seq')
All inputs are finite; a program needn't handle non-finite values.
Results may differ from a plain program's by a relative error of at most 0.001.
Values may be sent and summed in bfloat16 or wider, within the bound.
No kernel may reach another device: no remote copies, remote signals or barrier semaphores. Data moves between devices by JAX's collectives and lax.ppermute only.
A program may use at most 64 MiB of HBM per device.

v0:
```python
import math

import jax
import jax.numpy as jnp
from jax import lax
from jax.sharding import PartitionSpec as P


def product_hi(form, left, right):
    return jnp.einsum(form, left, right, precision=lax.Precision.HIGHEST)


def phase_of(numer, denom):
    angle = 2.0 * math.pi / denom * (numer % denom).astype(jnp.float32)
    return (jnp.cos(angle), jnp.sin(angle))


def local_conv(x, s, gain):
    count, length = x.shape
    full_len = 2 * length
    n1_len, n2_len = s.shape[2], s.shape[3]
    half1 = length // n2_len
    ids1 = jnp.arange(n1_len, dtype=jnp.int32)
    ids2 = jnp.arange(n2_len, dtype=jnp.int32)
    c1, s1 = phase_of(ids1[:, None] * ids1[None, :], n1_len)
    c2, s2 = phase_of(ids2[:, None] * ids2[None, :], n2_len)
    tc, ts = phase_of(ids1[:, None] * ids2[None, :], full_len)
    xr = x.reshape(count, half1, n2_len)
    ar = product_hi("kn,cnm->ckm", c1[:, :half1], xr)
    ai = -product_hi("kn,cnm->ckm", s1[:, :half1], xr)
    br = ar * tc + ai * ts
    bi = ai * tc - ar * ts
    xfr = product_hi("ckn,nj->ckj", br, c2) + product_hi("ckn,nj->ckj", bi, s2)
    xfi = product_hi("ckn,nj->ckj", bi, c2) - product_hi("ckn,nj->ckj", br, s2)
    pr = xfr * s[0] - xfi * s[1]
    pi = xfr * s[1] + xfi * s[0]
    qr = product_hi("ckj,jn->ckn", pr, c2) - product_hi("ckj,jn->ckn", pi, s2)
    qi = product_hi("ckj,jn->ckn", pi, c2) + product_hi("ckj,jn->ckn", pr, s2)
    rr = qr * tc - qi * ts
    ri = qi * tc + qr * ts
    y = product_hi("nk,ckm->cnm", c1[:half1], rr) - product_hi("nk,ckm->cnm", s1[:half1], ri)
    y = y.reshape(count, length) * (1.0 / full_len)
    return (y + gain[:, None] * x).astype(jnp.bfloat16)


def per_device(signal, spectrum, skip_gain):
    ch_blk, slab = signal.shape
    parts = lax.axis_size("seq")
    cpd = ch_blk // parts
    a_loc, nb = spectrum.shape[2], spectrum.shape[3]
    seq_rank = lax.axis_index("seq")
    sig = signal.reshape(parts, cpd, slab)
    spc = spectrum.reshape(2, parts, cpd, a_loc, nb).transpose(1, 2, 0, 3, 4)
    spc = spc.reshape(parts, cpd, 2 * a_loc * nb)
    buf = jnp.concatenate([sig, spc], axis=2)
    got = lax.all_to_all(buf, "seq", 0, 0, tiled=True)
    x = got[:, :, :slab].transpose(1, 0, 2).reshape(cpd, parts * slab).astype(jnp.float32)
    full_len = 2 * parts * slab
    n1_len = 1 << (int(math.log2(full_len)) // 2)
    n2_len = full_len // n1_len
    rep = n1_len // (parts * a_loc)
    cols = jnp.arange(nb, dtype=jnp.int32)
    perm = (cols[:, None] == (cols[None, :] % n2_len) * rep + cols[None, :] // n2_len)
    s = got[:, :, slab:].reshape(parts, cpd, 2, a_loc, nb)
    s = jnp.einsum("pcrab,bq->pcraq", s, perm.astype(jnp.bfloat16),
                   preferred_element_type=jnp.float32)
    s = s.reshape(parts, cpd, 2, a_loc, rep, n2_len).transpose(2, 1, 4, 0, 3, 5)
    s = s.reshape(2, cpd, n1_len, n2_len)
    gain = lax.dynamic_slice_in_dim(skip_gain, seq_rank * cpd, cpd)
    out = local_conv(x, s, gain)
    back = out.reshape(cpd, parts, slab).transpose(1, 0, 2)
    back = lax.all_to_all(back, "seq", 0, 0, tiled=True)
    return back.reshape(ch_blk, slab)


def solution(mesh):
    return jax.shard_map(
        per_device,
        mesh=mesh,
        in_specs=(P("chan", "seq"), P(None, "chan", "seq", None), P("chan")),
        out_specs=P("chan", "seq"),
        check_vma=False,
    )
```

profile of v0, /device:TPU:10, one launch (start us, length us, event | category | flops | bytes accessed | tf_op | source)
XLA Modules:
  0.0 139.0 jit_solution(8113954559252110594)
XLA Ops:
  0.0 0.0 copy-start.5
  0.0 2.2 %copy.96 = bf16[2,32,4,2,1024]{4,3,0,2,1:T(2,128)(2,1)S(1)} copy(bf16[2,32,4,2,1024]{4,3,2,1,0:T(2,128)(2,1)} %bitcast.65) | data formatting | bytes 2097152 | tf_op jit(solution)/shard_map/reshape | solution.py:53
  2.2 0.7 reshape.155
  2.9 0.0 copy-done.5
  2.9 0.1 reshape.153
  3.0 1.7 %pad_maximum_fusion = bf16[32,4,5120]{2,1,0:T(4,128)(2,1)} fusion(bf16[32,4,4096]{2,1,0:T(4,128)(2,1)S(1)} %reshape.155, bf16[32,4,1024]{2,1,0:T(4,128)(2,1)S(1)} %reshape.153), kind=kLoop, calls=%fused_computation.9 | loop fusion | flops 2621440 | bytes 2621440 | tf_op jit(solution)/shard_map/concatenate | solution.py:55
  4.7 0.0 copy-start.6
  4.7 15.6 %all-to-all-start = ((bf16[32,4,5120]{2,1,0:T(4,128)(2,1)}), bf16[32,4,5120]{2,1,0:T(4,128)(2,1)S(1)}, u32[]{:S(2)}, u32[]{:S(2)}) async-start(bf16[32,4,5120]{2,1,0:T(4,128)(2,1)} %pad_maximum_fusion), calls=%async_computation | async-start | bytes 2621440 | tf_op jit(solution)/shard_map/all_to_all | solution.py:56
  20.3 1.0 fusion.39
  21.3 0.1 copy.58
  21.4 1.0 fusion.40
  22.4 0.1 copy.56
  22.5 0.0 copy-done.6
  22.6 0.1 dynamic_slice.3
  22.6 1.0 fusion.41
  23.6 0.0 copy-start.3
  23.6 1.0 fusion.42
  24.6 1.6 %iota_compare_fusion = pred[1024,1024]{1,0:T(32,128)(4,1)} fusion(s32[1024]{0:T(1024)S(1)} %fusion.57), kind=kLoop, calls=%fused_computation | loop fusion | flops 1048576 | bytes 1052672 | tf_op jit(solution)/shard_map/eq | solution.py:63
  26.2 33.4 %all-to-all-done = bf16[32,4,5120]{2,1,0:T(4,128)(2,1)S(1)} async-done(((bf16[32,4,5120]{2,1,0:T(4,128)(2,1)}), bf16[32,4,5120]{2,1,0:T(4,128)(2,1)S(1)}, u32[]{:S(2)}, u32[]{:S(2)}) %all-to-all-start) | async-done | bytes 1310752 | tf_op jit(solution)/shard_map/all_to_all | solution.py:56
  59.6 0.0 copy-start
  59.6 0.1 slice.36
  59.7 0.1 copy.97
  59.8 0.9 copy-done
  60.7 0.2 reshape.156
  60.9 0.0 copy-done.3
  60.9 0.6 fusion
  61.5 0.6 convolution_bitcast_fusion.1
  62.1 3.7 %fusion.30 = f32[4,256,256]{2,1,0:T(8,128)} fusion(f32[4,256,256]{1,2,0:T(8,128)S(1)} %fusion, f32[4,256,256]{1,2,0:T(8,128)S(1)} %convolution_bitcast_fusion.1, f32[256,256]{0,1:T(8,128)S(1)} %copy.58, f32[256,256]{0,1:T(8,128)S(1)} %copy.56), kind=kOutput, calls=%fused_computation.52 | convolution fusion | flops 807010304 | bytes 3670016 | tf_op jit(solution)/shard_map/ckn,nj->ckj/dot_general | solution.py:10
  65.8 0.0 copy-start.1
  65.8 13.1 %fusion.28 = f32[4,256,256]{2,1,0:T(8,128)} fusion(f32[4,256,256]{1,2,0:T(8,128)S(1)} %convolution_bitcast_fusion.1, f32[4,256,256]{1,2,0:T(8,128)S(1)} %fusion, f32[256,256]{0,1:T(8,128)S(1)} %copy.58, f32[256,256]{0,1:T(8,128)S(1)} %copy.56), kind=kOutput, calls=%fused_computation.50 | convolution fusion | flops 807010304 | bytes 3670016 | tf_op jit(solution)/shard_map/ckn,nj->ckj/dot_general | solution.py:10
  79.0 0.0 copy-done.1
  79.0 1.5 %slice.39 = bf16[32,4,4096]{2,1,0:T(4,128)(2,1)} slice(bf16[32,4,5120]{2,1,0:T(4,128)(2,1)S(1)} %copy-done.1), slice={[0:32], [0:4], [1024:5120]} | slice | bytes 2097152 | tf_op jit(solution)/shard_map/slice | solution.py:64
  80.5 2.9 %reshape.167 = bf16[32,4,2,2,1024]{4,3,2,1,0:T(2,128)(2,1)} reshape(bf16[32,4,4096]{2,1,0:T(4,128)(2,1)} %slice.39) | data formatting | bytes 2097152 | tf_op jit(solution)/shard_map/reshape | solution.py:64
  83.4 3.0 %convolution_bitcast_fusion = f32[2,4,4,32,2,256]{5,3,2,4,0,1:T(8,128)S(1)} fusion(pred[4,256,1024,1,1,1]{2,1,0,5,4,3:T(32,128)(4,1)} %bitcast.66, bf16[32,4,2,2,1024,1]{4,3,2,1,0,5:T(2,128)(2,1)} %bitcast.67), kind=kOutput, calls=%fused_computation.1 | convolution fusion | flops 1073741824 | bytes 4194304 | tf_op jit(solution)/shard_map/pcrab,bq->pcraq/dot_general | solution.py:65
  86.4 1.2 fusion.92
  87.6 1.8 %copy.66 = f32[1,4,4,32,2,256]{5,4,3,2,1,0:T(2,128)} copy(f32[1,4,4,32,2,256]{5,3,2,4,0,1:T(8,128)S(1)} %get-tuple-element.7) | data formatting | bytes 2097152 | tf_op jit(solution)/shard_map/slice | solution.py:35
  89.3 2.9 %squeeze.9 = f32[4,256,256]{2,1,0:T(8,128)} reshape(f32[1,4,4,32,2,256]{5,4,3,2,1,0:T(2,128)} %copy.66) | data formatting | bytes 2097152 | tf_op jit(solution)/shard_map/squeeze | solution.py:35
  92.3 0.0 copy-start.2
  92.3 5.0 %convolution_add_fusion.1 = f32[4,256,256]{2,1,0:T(8,128)} fusion(f32[4,256,256]{2,1,0:T(8,128)} %fusion.30, f32[4,256,256]{1,2,0:T(8,128)S(1)} %convolution_bitcast_fusion.1, f32[4,256,256]{1,2,0:T(8,128)S(1)} %fusion, f32[256,256]{0,1:T(8,128)S(1)} %copy.58, f32[256,256]{0,1:T(8,128)S(1)} %copy.56), kind=kOutput, calls=%fused_computation.8 | convolution fusion | flops 807272448 | bytes 4718592 | tf_op jit(solution)/shard_map/ckn,nj->ckj/dot_general | solution.py:10
  97.3 0.0 copy-done.2
  97.3 1.8 %copy.63 = f32[1,4,4,32,2,256]{5,4,3,2,1,0:T(2,128)} copy(f32[1,4,4,32,2,256]{5,3,2,4,0,1:T(8,128)S(1)} %copy-done.2) | data formatting | bytes 2097152 | tf_op jit(solution)/shard_map/slice | solution.py:35
  99.1 2.9 %squeeze.8 = f32[4,256,256]{2,1,0:T(8,128)} reshape(f32[1,4,4,32,2,256]{5,4,3,2,1,0:T(2,128)} %copy.63) | data formatting | bytes 2097152 | tf_op jit(solution)/shard_map/squeeze | solution.py:35
  102.0 5.1 %multiply_subtract_fusion = (f32[4,256,256]{2,1,0:T(8,128)S(1)}, f32[4,256,256]{2,1,0:T(8,128)S(1)}) fusion(f32[4,256,256]{2,1,0:T(8,128)} %squeeze.9, f32[4,256,256]{2,1,0:T(8,128)} %convolution_add_fusion.1, f32[4,256,256]{2,1,0:T(8,128)} %squeeze.8, f32[4,256,256]{2,1,0:T(8,128)} %fusion.28, f32[4,256,256]{1,2,0:T(8,128)S(1)} %fusion, ...), kind=kOutput, calls=%fused_computation.23 | convolution fusion | flops 808845312 | bytes 8912896 | tf_op jit(solution)/shard_map/ckn,nj->ckj/dot_general | solution.py:10
  107.1 2.3 %fusion.24 = f32[4,256,256]{1,2,0:T(8,128)S(1)} fusion(f32[4,256,256]{2,1,0:T(8,128)S(1)} %get-tuple-element.6), kind=kOutput, calls=%fused_computation.46 | convolution fusion | flops 806223872 | bytes 2097152 | tf_op jit(solution)/shard_map/ckj,jn->ckn/dot_general | solution.py:10
  109.4 2.1 %fusion.26 = f32[4,256,256]{1,2,0:T(8,128)S(1)} fusion(f32[4,256,256]{2,1,0:T(8,128)S(1)} %get-tuple-element.5), kind=kOutput, calls=%fused_computation.48 | convolution fusion | flops 806223872 | bytes 2097152 | tf_op jit(solution)/shard_map/ckj,jn->ckn/dot_general | solution.py:10
  111.5 2.1 %convolution_add_fusion = f32[4,256,256]{1,2,0:T(8,128)S(1)} fusion(f32[4,256,256]{1,2,0:T(8,128)S(1)} %fusion.24, f32[4,256,256]{2,1,0:T(8,128)S(1)} %get-tuple-element.5), kind=kOutput, calls=%fused_computation.5 | convolution fusion | flops 806486016 | bytes 3145728 | tf_op jit(solution)/shard_map/ckj,jn->ckn/dot_general | solution.py:10
  113.6 2.1 %convolution_subtract_fusion = f32[4,256,256]{1,2,0:T(8,128)S(1)} fusion(f32[4,256,256]{1,2,0:T(8,128)S(1)} %fusion.26, f32[4,256,256]{2,1,0:T(8,128)S(1)} %get-tuple-element.6), kind=kOutput, calls=%fused_computation.6 | convolution fusion | flops 806486016 | bytes 3145728 | tf_op jit(solution)/shard_map/ckj,jn->ckn/dot_general | solution.py:10
  115.6 0.0 copy-start.4
  115.7 1.0 fusion.7
  116.7 0.0 copy-done.4
  116.7 1.0 fusion.2
  117.7 0.2 copy.71
  117.9 0.1 mul.338
  118.1 0.1 fusion.19
  118.2 0.2 copy.72
  118.4 19.6 %all_to_all.10 = bf16[32,4,1024]{2,1,0:T(4,128)(2,1)S(1)} all-to-all(bf16[32,4,1024]{2,1,0:T(4,128)(2,1)S(1)} %copy.72), channel_id=1, replica_groups=mesh['seq'=32,'chan'=16] {'seq'}, dimensions={0} | all-to-all | bytes 524288 | tf_op jit(solution)/shard_map/all_to_all | solution.py:72
  138.0 0.8 reshape.158
  (1 shorter events, 0.0 us)
Async XLA Ops:
  0.0 2.9 %copy-start.5 = (bf16[128,1024]{1,0:T(8,128)(2,1)S(1)}, bf16[128,1024]{1,0:T(8,128)(2,1)}, u32[]{:S(2)}) copy-start(bf16[128,1024]{1,0:T(8,128)(2,1)} %param.3) | copy-start | bytes 786436
  4.7 17.8 %copy-start.6 = (f32[128]{0:T(128)S(1)}, f32[128]{0:T(128)}, u32[]{:S(2)}) copy-start(f32[128]{0:T(128)} %param.5) | copy-start | bytes 1540
  4.7 54.9 %all-to-all-start = ((bf16[32,4,5120]{2,1,0:T(4,128)(2,1)}), bf16[32,4,5120]{2,1,0:T(4,128)(2,1)S(1)}, u32[]{:S(2)}, u32[]{:S(2)}) async-start(bf16[32,4,5120]{2,1,0:T(4,128)(2,1)} %pad_maximum_fusion), calls=%async_computation | async-start | bytes 2621440 | tf_op jit(solution)/shard_map/all_to_all | solution.py:56
  23.6 37.2 %copy-start.3 = (f32[256,256]{1,0:T(8,128)}, f32[256,256]{1,0:T(8,128)S(1)}, u32[]{:S(2)}) copy-start(f32[256,256]{1,0:T(8,128)S(1)} %fusion.41) | copy-start | bytes 786436
  59.6 1.1 copy-start
  65.8 13.1 %copy-start.1 = (bf16[32,4,5120]{2,1,0:T(4,128)(2,1)S(1)}, bf16[32,4,5120]{2,1,0:T(4,128)(2,1)}, u32[]{:S(2)}) copy-start(bf16[32,4,5120]{2,1,0:T(4,128)(2,1)} %copy-done) | copy-start | bytes 3932164
  92.3 5.0 %copy-start.2 = (f32[1,4,4,32,2,256]{5,3,2,4,0,1:T(8,128)S(1)}, f32[1,4,4,32,2,256]{5,3,2,4,0,1:T(8,128)}, u32[]{:S(2)}) copy-start(f32[1,4,4,32,2,256]{5,3,2,4,0,1:T(8,128)} %get-tuple-element.8) | copy-start | bytes 3145732
  115.6 1.0 copy-start.4
where the time goes:
time: 142 us; the launch traced here: 139 us
  matrix products  41.7 us (29%)
  waiting for transfers between devices  33.4 us (24%)
  local copies, waits for them, and re-layouts  20.9 us (15%)
  blocking collectives  19.6 us (14%)
  starting transfers between devices  15.6 us (11%)
  other arithmetic  7.37 us (5%)
    dot_general x12, matrix products, product_hi(): return jnp.einsum(form, left, right, precision=lax.Precision.HIGHEST)  38.7 us
    all_to_all x1, waiting for transfers between devices, per_device(): got = lax.all_to_all(buf, 'seq', 0, 0, tiled=True)  33.4 us
    all_to_all x1, blocking collectives, per_device(): back = lax.all_to_all(back, 'seq', 0, 0, tiled=True)  19.6 us
    all_to_all x1, starting transfers between devices, per_device(): got = lax.all_to_all(buf, 'seq', 0, 0, tiled=True)  15.6 us
    squeeze x2, local copies, waits for them, and re-layouts, local_conv(): pr = xfr * s[0] - xfi * s[1]  5.86 us
    slice x3, local copies, waits for them, and re-layouts, local_conv(): pr = xfr * s[0] - xfi * s[1]  4.72 us
    dot_general x1, matrix products, per_device(): jnp.einsum('pcrab,bq->pcraq', s, perm.astype(jnp.bfloat16), preferred_ele...  2.97 us
    reshape x1, local copies, waits for them, and re-layouts, per_device(): s = got[:, :, slab:].reshape(parts, cpd, 2, a_loc, nb)  2.92 us
  transfers between devices with their start and end apart: 1, of which 1 were waited for; matrix products, arithmetic and copies ran while one was open for 4% of the time, Pallas kernels for 0%

commit v1 on v0

v1 whole, which is shorter than its diff:
```python
import math

import jax
import jax.numpy as jnp
from jax import lax
from jax.sharding import PartitionSpec as P


def dot_hi(form, left, right):
    return jnp.einsum(form, left, right, precision=lax.Precision.HIGH,
                      preferred_element_type=jnp.float32)


def angle_of(numer, denom):
    return 2.0 * math.pi / denom * (numer % denom).astype(jnp.float32)


def local_conv(x, s, gain, n1_len, km):
    count, length = x.shape
    full_len = 2 * length
    n2_len = full_len // n1_len
    half1 = length // n2_len
    rep = n1_len // km
    rows = jnp.arange(n1_len, dtype=jnp.int32)
    k1 = rows // rep + km * (rows % rep)
    ids2 = jnp.arange(n2_len, dtype=jnp.int32)
    n1 = jnp.arange(half1, dtype=jnp.int32)
    angles = jnp.concatenate([
        angle_of(k1[:, None] * jnp.pad(n1, (0, n2_len - half1))[None, :], n1_len),
        angle_of(ids2[:, None] * ids2[None, :], n2_len),
        angle_of(k1[:, None] * ids2[None, :], full_len),
    ], axis=0)
    tab_c, tab_s = lax.optimization_barrier((jnp.cos(angles), jnp.sin(angles)))
    f1c, f1s = tab_c[:n1_len, :half1], tab_s[:n1_len, :half1]
    wc, ws = tab_c[n1_len:n1_len + n2_len], tab_s[n1_len:n1_len + n2_len]
    tc, ts = tab_c[n1_len + n2_len:], tab_s[n1_len + n2_len:]
    xr = x.reshape(count, half1, n2_len)
    f1 = jnp.stack([f1c, -f1s])
    a = dot_hi("zkn,cnm->zckm", f1, xr)
    ar, ai = a[0], a[1]
    br = ar * tc + ai * ts
    bi = ai * tc - ar * ts
    w = jnp.stack([wc, ws])
    xf = dot_hi("zckn,wnj->zwckj", jnp.stack([br, bi]), w)
    xfr = xf[0, 0] + xf[1, 1]
    xfi = xf[1, 0] - xf[0, 1]
    pr = xfr * s[0] - xfi * s[1]
    pi = xfr * s[1] + xfi * s[0]
    q = dot_hi("zckj,wjn->zwckn", jnp.stack([pr, pi]), w)
    qr = q[0, 0] - q[1, 1]
    qi = q[1, 0] + q[0, 1]
    rr = qr * tc - qi * ts
    ri = qi * tc + qr * ts
    y = dot_hi("zkn,zckm->cnm", jnp.stack([f1c, -f1s]), jnp.stack([rr, ri]))
    y = y.reshape(count, length) * (1.0 / full_len)
    return (y + gain[:, None] * x).astype(jnp.bfloat16)


def per_device(signal, spectrum, skip_gain):
    ch_blk, slab = signal.shape
    parts = lax.axis_size("seq")
    cpd = ch_blk // parts
    a_loc, nb = spectrum.shape[2], spectrum.shape[3]
    km = parts * a_loc
    full_len = 2 * parts * slab
    n1_len = 1 << (int(math.log2(full_len)) // 2)
    n2_len = full_len // n1_len
    rep = n1_len // km
    seq_rank = lax.axis_index("seq")
    sig = signal.reshape(parts, cpd, 1, slab)
    spc = spectrum.reshape(2, parts, cpd, a_loc, nb).transpose(1, 2, 0, 3, 4)
    spc = spc.reshape(parts, cpd, 2 * a_loc, nb)
    buf = jnp.concatenate([sig, spc], axis=2)
    got = lax.all_to_all(buf, "seq", 0, 0, tiled=True)
    x = got[:, :, 0].transpose(1, 0, 2).reshape(cpd, parts * slab).astype(jnp.float32)
    cols = jnp.arange(nb, dtype=jnp.int32)
    perm = cols[:, None] == (cols[None, :] % n2_len) * rep + cols[None, :] // n2_len
    s = jnp.einsum("pcrb,bq->pcrq", got[:, :, 1:], perm.astype(jnp.bfloat16),
                   preferred_element_type=jnp.float32)
    s = s.reshape(parts, cpd, 2, a_loc, nb).transpose(2, 1, 0, 3, 4)
    s = s.reshape(2, cpd, n1_len, n2_len)
    gain = lax.dynamic_slice_in_dim(skip_gain, seq_rank * cpd, cpd)
    out = local_conv(x, s, gain, n1_len, km)
    back = out.reshape(cpd, parts, slab).transpose(1, 0, 2)
    back = lax.all_to_all(back, "seq", 0, 0, tiled=True)
    return back.reshape(ch_blk, slab)


def solution(mesh):
    return jax.shard_map(
        per_device,
        mesh=mesh,
        in_specs=(P("chan", "seq"), P(None, "chan", "seq", None), P("chan")),
        out_specs=P("chan", "seq"),
        check_vma=False,
    )
```

time: 142 us -> 101 us (0.71)
  the two profiles are of different devices: /device:TPU:10 before, /device:TPU:14 now
where the time goes in v1:
time: 101 us; the launch traced here: 100 us
  waiting for transfers between devices  32.3 us (32%)
  blocking collectives  19.6 us (19%)
  local copies, waits for them, and re-layouts  17.4 us (17%)
  starting transfers between devices  15.1 us (15%)
  matrix products  9.04 us (9%)
  other arithmetic  6.48 us (6%)
    all_to_all x1, waiting for transfers between devices, per_device(): got = lax.all_to_all(buf, 'seq', 0, 0, tiled=True)  32.3 us
    all_to_all x1, blocking collectives, per_device(): back = lax.all_to_all(back, 'seq', 0, 0, tiled=True)  19.6 us
    all_to_all x1, starting transfers between devices, per_device(): got = lax.all_to_all(buf, 'seq', 0, 0, tiled=True)  15.1 us
    dot_general x4, matrix products, dot_hi(): jnp.einsum(form, left, right, precision=lax.Precision.HIGH, preferred_ele...  6.92 us
    squeeze x4, local copies, waits for them, and re-layouts, local_conv(): pr = xfr * s[0] - xfi * s[1]  4.55 us
    sin x1, other arithmetic, local_conv(): tab_c, tab_s = lax.optimization_barrier((jnp.cos(angles), jnp.sin(angles)))  2.93 us
    dot_general x1, matrix products, per_device(): jnp.einsum('pcrb,bq->pcrq', got[:, :, 1:], perm.astype(jnp.bfloat16), pre...  2.12 us
  transfers between devices with their start and end apart: 1, of which 1 were waited for; matrix products, arithmetic and copies ran while one was open for 7% of the time, Pallas kernels for 0%

profile of v1, /device:TPU:14, one launch (start us, length us, event | category | flops | bytes accessed | tf_op | source)
XLA Modules:
  0.0 100.3 jit_solution(5133453465053354772)
XLA Ops:
  0.0 0.0 copy-start.6
  0.0 1.8 %copy.74 = bf16[2,32,4,2,1024]{4,2,3,0,1:T(4,128)(2,1)S(1)} copy(bf16[2,32,4,2,1024]{4,3,2,1,0:T(2,128)(2,1)} %bitcast.120) | data formatting | bytes 2097152 | tf_op jit(solution)/shard_map/reshape | solution.py:71
  1.8 0.0 copy-done.6
  1.8 0.1 reshape.284
  1.9 0.0 copy-start.7
  2.0 1.9 %pad_maximum_fusion = bf16[32,4,5,1024]{3,1,2,0:T(4,128)(2,1)} fusion(bf16[32,4,4,1024]{3,1,2,0:T(4,128)(2,1)S(1)} %bitcast.117, bf16[32,4,1,1024]{3,1,2,0:T(4,128)(2,1)S(1)} %bitcast.119), kind=kLoop, calls=%fused_computation.17 | loop fusion | flops 655360 | bytes 2621440 | tf_op jit(solution)/shard_map/concatenate | solution.py:73
  3.9 15.1 %all-to-all-start = ((bf16[32,4,5,1024]{3,1,2,0:T(4,128)(2,1)}), bf16[32,4,5,1024]{3,1,2,0:T(4,128)(2,1)S(1)}, u32[]{:S(2)}, u32[]{:S(2)}) async-start(bf16[32,4,5,1024]{3,1,2,0:T(4,128)(2,1)} %pad_maximum_fusion), calls=%async_computation | async-start | bytes 2621440 | tf_op jit(solution)/shard_map/all_to_all | solution.py:74
  19.0 0.0 copy-done.7
  19.0 0.4 fusion.31
  19.4 2.9 %fusion.26 = (f32[768,256]{1,0:T(8,128)S(1)}, f32[768,256]{1,0:T(8,128)S(1)}) fusion(f32[256,256]{1,0:T(8,128)S(1)} %get-tuple-element.24, f32[256,256]{1,0:T(8,128)S(1)} %get-tuple-element.25, f32[256,256]{1,0:T(8,128)S(1)} %get-tuple-element.23), kind=kLoop, calls=%fused_computation.39 | loop fusion | flops 393216 | bytes 2359296 | tf_op jit(solution)/shard_map/sin | solution.py:33
  22.4 0.0 copy-start.8
  22.4 0.7 slice_bitcast_fusion.2
  23.1 0.8 copy.79
  24.0 0.7 slice_bitcast_fusion.3
  24.7 0.9 copy.78
  25.5 0.0 copy-done.8
  25.5 0.1 dynamic_slice.3
  25.6 0.7 slice_bitcast_fusion.4
  26.3 32.3 %all-to-all-done = bf16[32,4,5,1024]{3,1,2,0:T(4,128)(2,1)S(1)} async-done(((bf16[32,4,5,1024]{3,1,2,0:T(4,128)(2,1)}), bf16[32,4,5,1024]{3,1,2,0:T(4,128)(2,1)S(1)}, u32[]{:S(2)}, u32[]{:S(2)}) %all-to-all-start) | async-done | bytes 1310752 | tf_op jit(solution)/shard_map/all_to_all | solution.py:74
  58.7 0.6 slice.89
  59.2 2.1 %fusion.1 = f32[32,4,4,1024]{3,0,2,1:T(8,128)S(1)} fusion(s32[1024]{0:T(1024)S(1)} %fusion.53, bf16[32,4,4,1024]{3,1,2,0:T(4,128)(2,1)S(1)} %slice.89), kind=kOutput, calls=%fused_computation.2 | convolution fusion | flops 1074790400 | bytes 3149824 | tf_op jit(solution)/shard_map/pcrb,bq->pcrq/dot_general | solution.py:78
  61.3 1.6 %copy.125 = f32[32,4,2,2,1024]{4,3,0,1,2:T(2,128)S(1)} copy(f32[32,4,2,2,1024]{4,0,3,2,1:T(8,128)S(1)} %bitcast.118) | data formatting | bytes 4194304 | tf_op jit(solution)/shard_map/reshape | solution.py:80
  63.0 1.9 %fusion.64 = (f32[1,4,32,2,1024]{4,3,2,1,0:T(2,128)}, f32[1,4,32,2,1024]{4,3,2,1,0:T(2,128)S(1)}) fusion(f32[2,4,32,2,1024]{4,3,2,1,0:T(2,128)S(1)} %bitcast.116), kind=kLoop, calls=%fused_computation.105 | loop fusion | bytes 4194304 | tf_op jit(solution)/shard_map/slice | solution.py:47
  64.9 2.1 %squeeze.8 = f32[1,4,256,256]{3,2,1,0:T(8,128)S(1)} reshape(f32[1,4,32,2,1024]{4,3,2,1,0:T(2,128)} %get-tuple-element.15) | data formatting | bytes 2097152 | tf_op jit(solution)/shard_map/squeeze | solution.py:47
  66.9 1.3 %copy.87 = f32[1,4,256,256]{2,3,1,0:T(8,128)} copy(f32[1,4,256,256]{3,2,1,0:T(8,128)S(1)} %squeeze.8) | data formatting | bytes 2097152 | tf_op jit(solution)/shard_map/squeeze | solution.py:47
  68.3 0.8 squeeze.7
  69.1 0.3 copy.86
  69.4 0.0 copy-start.1
  69.5 0.0 copy-start.2
  69.5 0.1 slice.84
  69.6 0.1 copy.126
  69.7 0.2 reshape.287
  69.8 1.7 %convolution_bitcast_fusion.2 = f32[2,4,256,256]{2,3,0,1:T(8,128)S(1)} fusion(bf16[4,128,256]{2,1,0:T(8,128)(2,1)S(1)} %reshape.287, f32[1,256,128]{2,1,0:T(8,128)S(1)} %negate_bitcast_fusion, f32[1,256,128]{2,1,0:T(8,128)} %slice_bitcast_fusion.4), kind=kOutput, calls=%fused_computation.16 | convolution fusion | flops 402718720 | bytes 2621440 | tf_op jit(solution)/shard_map/zkn,cnm->zckm/dot_general | solution.py:10
  71.5 0.0 copy-done.1
  71.5 0.0 copy-done.2
  71.5 0.0 copy-start.3
  71.5 0.0 copy-start.4
  71.5 0.3 multiply_add_fusion.2
  71.8 0.6 copy-done.3
  72.5 0.1 copy-done.4
  72.6 0.0 copy-start
  72.6 2.0 %convolution_bitcast_fusion.1 = f32[2,2,4,256,256]{3,4,2,0,1:T(8,128)S(1)} fusion(f32[1,256,256]{2,1,0:T(8,128)S(1)} %copy-done.3, f32[1,256,256]{2,1,0:T(8,128)S(1)} %copy-done.4, f32[1,4,256,256]{2,3,0,1:T(8,128)S(1)} %get-tuple-element.14, f32[1,4,256,256]{2,3,0,1:T(8,128)S(1)} %get-tuple-element.13), kind=kOutput, calls=%fused_computation.4 | convolution fusion | flops 1611268096 | bytes 6815744 | tf_op jit(solution)/shard_map/zckn,wnj->zwckj/dot_general | solution.py:10
  74.6 0.0 copy-done
  74.6 0.4 multiply_subtract_fusion.1
  75.0 2.3 %convolution_bitcast_fusion = f32[2,2,4,256,256]{3,4,2,1,0:T(8,128)S(1)} fusion(f32[1,4,256,256]{2,3,1,0:T(8,128)S(1)} %get-tuple-element.10, f32[1,4,256,256]{2,3,1,0:T(8,128)S(1)} %get-tuple-element.9, f32[1,256,256]{2,1,0:T(8,128)S(1)} %copy-done.3, f32[1,256,256]{2,1,0:T(8,128)S(1)} %copy-done.4), kind=kOutput, calls=%fused_computation.3 | convolution fusion | flops 1611268096 | bytes 6815744 | tf_op jit(solution)/shard_map/zckj,wjn->zwckn/dot_general | solution.py:10
  77.3 0.0 copy-start.5
  77.3 0.3 multiply_subtract_fusion
  77.6 0.6 copy-done.5
  78.2 1.0 fusion.17
  79.2 0.2 copy.93
  79.4 0.1 mul.256
  79.5 0.1 fusion.39
  79.7 0.2 copy.94
  79.9 19.6 %all_to_all.10 = bf16[32,4,1024]{2,1,0:T(4,128)(2,1)S(1)} all-to-all(bf16[32,4,1024]{2,1,0:T(4,128)(2,1)S(1)} %copy.94), channel_id=1, replica_groups=mesh['seq'=32,'chan'=16] {'seq'}, dimensions={0} | all-to-all | bytes 524288 | tf_op jit(solution)/shard_map/all_to_all | solution.py:85
  99.5 0.8 reshape.289
  (3 shorter events, 0.0 us)
Async XLA Ops:
  0.0 1.8 %copy-start.6 = (bf16[128,1024]{1,0:T(8,128)(2,1)S(1)}, bf16[128,1024]{1,0:T(8,128)(2,1)}, u32[]{:S(2)}) copy-start(bf16[128,1024]{1,0:T(8,128)(2,1)} %param.3) | copy-start | bytes 786436
  1.9 17.0 %copy-start.7 = (s32[256]{0:T(256)S(1)}, s32[256]{0:T(256)}, u32[]{:S(2)}) copy-start(s32[256]{0:T(256)} %constant.91.clone.1) | copy-start | bytes 3076
  3.9 54.8 %all-to-all-start = ((bf16[32,4,5,1024]{3,1,2,0:T(4,128)(2,1)}), bf16[32,4,5,1024]{3,1,2,0:T(4,128)(2,1)S(1)}, u32[]{:S(2)}, u32[]{:S(2)}) async-start(bf16[32,4,5,1024]{3,1,2,0:T(4,128)(2,1)} %pad_maximum_fusion), calls=%async_computation | async-start | bytes 2621440 | tf_op jit(solution)/shard_map/all_to_all | solution.py:74
  22.4 3.2 %copy-start.8 = (f32[128]{0:T(128)S(1)}, f32[128]{0:T(128)}, u32[]{:S(2)}) copy-start(f32[128]{0:T(128)} %param.5) | copy-start | bytes 1540
  69.4 2.1 %copy-start.1 = (f32[256,256]{0,1:T(8,128)S(1)}, f32[256,256]{0,1:T(8,128)}, u32[]{:S(2)}) copy-start(f32[256,256]{0,1:T(8,128)} %copy.79) | copy-start | bytes 786436
  69.5 2.1 %copy-start.2 = (f32[256,256]{0,1:T(8,128)S(1)}, f32[256,256]{0,1:T(8,128)}, u32[]{:S(2)}) copy-start(f32[256,256]{0,1:T(8,128)} %copy.78) | copy-start | bytes 786436
  71.5 1.0 copy-start.3
  71.5 1.0 %copy-start.4 = (f32[1,256,256]{2,1,0:T(8,128)S(1)}, f32[1,256,256]{2,1,0:T(8,128)}, u32[]{:S(2)}) copy-start(f32[1,256,256]{2,1,0:T(8,128)} %get-tuple-element.17) | copy-start | bytes 786436
  72.6 2.0 %copy-start = (f32[1,4,256,256]{2,3,1,0:T(8,128)S(1)}, f32[1,4,256,256]{2,3,1,0:T(8,128)}, u32[]{:S(2)}) copy-start(f32[1,4,256,256]{2,3,1,0:T(8,128)} %copy.87) | copy-start | bytes 3145732
  77.3 0.9 copy-start.5

commit v2 on v1

--- a/solution.py
+++ b/solution.py
@@ -36,8 +36,12 @@
     tc, ts = tab_c[n1_len + n2_len:], tab_s[n1_len + n2_len:]
     xr = x.reshape(count, half1, n2_len)
     f1 = jnp.stack([f1c, -f1s])
-    a = dot_hi("zkn,cnm->zckm", f1, xr)
-    ar, ai = a[0], a[1]
+    f1_top = lax.reduce_precision(f1, exponent_bits=8, mantissa_bits=7)
+    f1_hi = f1_top.astype(jnp.bfloat16)
+    f1_lo = (f1 - f1_top).astype(jnp.bfloat16)
+    a = jnp.einsum("hzkn,cnm->hzckm", jnp.stack([f1_hi, f1_lo]), xr,
+                   preferred_element_type=jnp.float32)
+    ar, ai = a[0, 0] + a[1, 0], a[0, 1] + a[1, 1]
     br = ar * tc + ai * ts
     bi = ai * tc - ar * ts
     w = jnp.stack([wc, ws])
@@ -53,7 +57,7 @@
     ri = qi * tc + qr * ts
     y = dot_hi("zkn,zckm->cnm", jnp.stack([f1c, -f1s]), jnp.stack([rr, ri]))
     y = y.reshape(count, length) * (1.0 / full_len)
-    return (y + gain[:, None] * x).astype(jnp.bfloat16)
+    return (y + gain[:, None] * x.astype(jnp.float32)).astype(jnp.bfloat16)
 
 
 def per_device(signal, spectrum, skip_gain):
@@ -67,18 +71,18 @@
     n2_len = full_len // n1_len
     rep = n1_len // km
     seq_rank = lax.axis_index("seq")
+    cols = jnp.arange(nb, dtype=jnp.int32)
+    perm = cols[:, None] == (cols[None, :] % n2_len) * rep + cols[None, :] // n2_len
+    spc = jnp.einsum("rcab,bq->rcaq", spectrum, perm.astype(jnp.bfloat16),
+                     preferred_element_type=jnp.float32).astype(jnp.bfloat16)
+    spc = spc.reshape(2, parts, cpd, a_loc, nb).transpose(1, 2, 0, 3, 4)
+    spc = spc.reshape(parts, cpd, 2 * a_loc, nb)
     sig = signal.reshape(parts, cpd, 1, slab)
-    spc = spectrum.reshape(2, parts, cpd, a_loc, nb).transpose(1, 2, 0, 3, 4)
-    spc = spc.reshape(parts, cpd, 2 * a_loc, nb)
     buf = jnp.concatenate([sig, spc], axis=2)
     got = lax.all_to_all(buf, "seq", 0, 0, tiled=True)
-    x = got[:, :, 0].transpose(1, 0, 2).reshape(cpd, parts * slab).astype(jnp.float32)
-    cols = jnp.arange(nb, dtype=jnp.int32)
-    perm = cols[:, None] == (cols[None, :] % n2_len) * rep + cols[None, :] // n2_len
-    s = jnp.einsum("pcrb,bq->pcrq", got[:, :, 1:], perm.astype(jnp.bfloat16),
-                   preferred_element_type=jnp.float32)
-    s = s.reshape(parts, cpd, 2, a_loc, nb).transpose(2, 1, 0, 3, 4)
-    s = s.reshape(2, cpd, n1_len, n2_len)
+    x = got[:, :, 0].transpose(1, 0, 2).reshape(cpd, parts * slab)
+    s = got[:, :, 1:].reshape(parts, cpd, 2, a_loc, rep, n2_len).astype(jnp.float32)
+    s = s.transpose(2, 1, 0, 3, 4, 5).reshape(2, cpd, n1_len, n2_len)
     gain = lax.dynamic_slice_in_dim(skip_gain, seq_rank * cpd, cpd)
     out = local_conv(x, s, gain, n1_len, km)
     back = out.reshape(cpd, parts, slab).transpose(1, 0, 2)

time: 101 us -> 101 us (level)
  other arithmetic: 6.48 us -> 9.63 us
  waiting for transfers between devices: 32.3 us -> 30 us
    reshape x3 -> x1, local copies, waits for them, and re-layouts: 3.6 us -> 0.43 us  [per_device(): spc = spc.reshape(2, parts, cpd, a_loc, nb).transpose(1, 2, 0, 3, 4)]
    transpose x0 -> x2, local copies, waits for them, and re-layouts: none -> 2.98 us  [the longest x1 2.38 us: per_device(): s = s.transpose(2, 1, 0, 3, 4, 5).reshape(2, cpd, n1_len, n2_len)]
    squeeze x4 -> x2, local copies, waits for them, and re-layouts: 4.55 us -> 1.77 us  [local_conv(): pr = xfr * s[0] - xfi * s[1]]
    all_to_all x1, waiting for transfers between devices: 32.3 us -> 30 us  [per_device(): got = lax.all_to_all(buf, 'seq', 0, 0, tiled=True)]
    unnamed x19 -> x25, local copies, waits for them, and re-layouts: 1.4 us -> 3.48 us
    dot_general x4 -> x3, matrix products: 6.92 us -> 4.91 us  [dot_hi(): jnp.einsum(form, left, right, precision=lax.Precision.HIGH, preferred_ele...]
    transpose x0 -> x1, other arithmetic: none -> 1.95 us  [per_device(): s = s.transpose(2, 1, 0, 3, 4, 5).reshape(2, cpd, n1_len, n2_len)]
    dot_general x1 -> x2, matrix products: 2.12 us -> 3.17 us  [the longest x1 1.83 us: local_conv(): jnp.einsum('hzkn,cnm->hzckm', jnp.stack([f1_hi, f1_lo]), xr, preferred_el...]
  transfers between devices with their start and end apart: 1 -> 1, of which waited for: 1 -> 1; matrix products, arithmetic and copies ran while one was open for 7% -> 9% of each run, Pallas kernels for 0% -> 0%
where the time goes in v2:
time: 101 us
  waiting for transfers between devices  30 us (30%)
  blocking collectives  19.6 us (19%)
  local copies, waits for them, and re-layouts  18.4 us (18%)
  starting transfers between devices  15.1 us (15%)
  other arithmetic  9.63 us (10%)
  matrix products  8.08 us (8%)
    all_to_all x1, waiting for transfers between devices, per_device(): got = lax.all_to_all(buf, 'seq', 0, 0, tiled=True)  30 us
    all_to_all x1, blocking collectives, per_device(): back = lax.all_to_all(back, 'seq', 0, 0, tiled=True)  19.6 us
    all_to_all x1, starting transfers between devices, per_device(): got = lax.all_to_all(buf, 'seq', 0, 0, tiled=True)  15.1 us
    dot_general x3, matrix products, dot_hi(): jnp.einsum(form, left, right, precision=lax.Precision.HIGH, preferred_ele...  4.91 us
    unnamed x25, local copies, waits for them, and re-layouts  3.48 us
    sin x1, other arithmetic, local_conv(): tab_c, tab_s = lax.optimization_barrier((jnp.cos(angles), jnp.sin(angles)))  2.75 us
    slice x3, local copies, waits for them, and re-layouts, local_conv(): pr = xfr * s[0] - xfi * s[1]  2.69 us
    transpose x1, local copies, waits for them, and re-layouts, per_device(): s = s.transpose(2, 1, 0, 3, 4, 5).reshape(2, cpd, n1_len, n2_len)  2.38 us
  transfers between devices with their start and end apart: 1, of which 1 were waited for; matrix products, arithmetic and copies ran while one was open for 9% of the time, Pallas kernels for 0%

profile of v2, /device:TPU:14, one launch (start us, length us, event | category | flops | bytes accessed | tf_op | source)
XLA Modules:
  0.0 101.1 jit_solution(3118954993567055407)
XLA Ops:
  0.0 0.0 copy-start
  0.0 1.2 %copy-done = bf16[2,128,2,1024]{3,2,1,0:T(2,128)(2,1)S(1)} copy-done((bf16[2,128,2,1024]{3,2,1,0:T(2,128)(2,1)S(1)}, bf16[2,128,2,1024]{3,2,1,0:T(2,128)(2,1)}, u32[]{:S(2)}) %copy-start) | copy-done | bytes 1048600
  1.2 1.3 %fusion.15 = bf16[2,128,2,1024]{3,1,2,0:T(8,128)(2,1)S(1)} fusion(s32[1024]{0:T(1024)S(1)} %fusion.70, bf16[2,128,2,1024]{3,2,1,0:T(2,128)(2,1)S(1)} %copy-done), kind=kOutput, calls=%fused_computation.18 | convolution fusion | flops 1075314688 | bytes 2101248 | tf_op jit(solution)/shard_map/rcab,bq->rcaq/dot_general | solution.py:76
  2.6 0.0 copy-start.9
  2.6 0.4 reshape.431
  3.0 0.6 copy.90
  3.6 0.0 copy-done.9
  3.6 0.1 reshape.430
  3.7 0.0 copy-start.10
  3.8 1.9 %pad_maximum_fusion = bf16[32,4,5,1024]{3,1,2,0:T(4,128)(2,1)} fusion(bf16[32,4,4,1024]{3,1,2,0:T(4,128)(2,1)S(1)} %bitcast.164, bf16[32,4,1,1024]{3,1,2,0:T(4,128)(2,1)S(1)} %bitcast.168), kind=kLoop, calls=%fused_computation.19 | loop fusion | flops 655360 | bytes 2621440 | tf_op jit(solution)/shard_map/concatenate | solution.py:81
  5.7 15.1 %all-to-all-start = ((bf16[32,4,5,1024]{3,1,2,0:T(4,128)(2,1)}), bf16[32,4,5,1024]{3,1,2,0:T(4,128)(2,1)S(1)}, u32[]{:S(2)}, u32[]{:S(2)}) async-start(bf16[32,4,5,1024]{3,1,2,0:T(4,128)(2,1)} %pad_maximum_fusion), calls=%async_computation | async-start | bytes 2621440 | tf_op jit(solution)/shard_map/all_to_all | solution.py:82
  20.8 0.0 copy-done.10
  20.8 0.4 fusion.42
  21.2 2.8 %fusion.36 = (f32[768,256]{1,0:T(8,128)S(1)}, f32[768,256]{1,0:T(8,128)S(1)}) fusion(f32[256,256]{1,0:T(8,128)S(1)} %get-tuple-element.30, f32[256,256]{1,0:T(8,128)S(1)} %get-tuple-element.31, f32[256,256]{1,0:T(8,128)S(1)} %get-tuple-element.29), kind=kLoop, calls=%fused_computation.48 | loop fusion | flops 393216 | bytes 2359296 | tf_op jit(solution)/shard_map/sin | solution.py:33
  24.0 0.0 copy-start.3
  24.0 0.0 copy-start.11
  24.0 0.9 copy-done.3
  24.8 0.7 slice_bitcast_fusion.5
  25.6 0.8 copy.96
  26.4 0.7 slice_bitcast_fusion.4
  27.2 0.8 copy.97
  28.0 0.0 copy-done.11
  28.0 0.1 dynamic_slice.3
  28.1 0.9 slice_bitcast_fusion.6
  29.0 0.7 fusion.62
  29.7 0.7 reduce-precision_convert_fusion
  30.4 30.0 %all-to-all-done = bf16[32,4,5,1024]{3,1,2,0:T(4,128)(2,1)S(1)} async-done(((bf16[32,4,5,1024]{3,1,2,0:T(4,128)(2,1)}), bf16[32,4,5,1024]{3,1,2,0:T(4,128)(2,1)S(1)}, u32[]{:S(2)}, u32[]{:S(2)}) %all-to-all-start) | async-done | bytes 1310752 | tf_op jit(solution)/shard_map/all_to_all | solution.py:82
  60.4 0.1 slice.92
  60.5 0.1 copy.143
  60.6 0.9 reshape_reshape.3
  61.5 0.5 slice.99
  62.0 2.0 %copy_convert_fusion = f32[32,4,4,1024]{3,0,2,1:T(8,128)} fusion(bf16[32,4,4,1024]{3,1,2,0:T(4,128)(2,1)S(1)} %slice.99), kind=kLoop, calls=%fused_computation.39 | loop fusion | flops 524288 | bytes 3145728 | tf_op jit(solution)/shard_map/transpose | solution.py:85
  64.0 2.4 %reshape.434 = f32[32,4,2,2,4,256]{5,4,0,3,2,1:T(4,128)S(1)} reshape(f32[32,4,4,1024]{3,0,2,1:T(8,128)} %copy_convert_fusion) | data formatting | bytes 4194304 | tf_op jit(solution)/shard_map/transpose | solution.py:85
  66.4 1.3 %fusion.81 = (f32[1,4,32,2,4,256]{5,4,2,3,0,1:T(4,128)}, f32[1,4,32,2,4,256]{5,4,2,3,0,1:T(4,128)S(1)}) fusion(f32[2,4,32,2,4,256]{5,4,2,3,0,1:T(4,128)S(1)} %bitcast.163), kind=kLoop, calls=%fused_computation.126 | loop fusion | bytes 4194304 | tf_op jit(solution)/shard_map/slice | solution.py:51
  67.7 0.0 copy-start.1
  67.7 0.7 copy.103
  68.4 1.4 %copy.104 = f32[1,4,256,256]{2,3,1,0:T(8,128)} copy(f32[1,4,256,256]{3,1,2,0:T(4,128)S(1)} %bitcast.166) | data formatting | bytes 2097152 | tf_op jit(solution)/shard_map/squeeze | solution.py:51
  69.8 0.0 copy-done.1
  69.8 0.7 copy.105
  70.5 0.4 copy.106
  70.8 0.0 copy-start.4
  70.9 0.0 copy-start.5
  70.9 1.8 %convolution_bitcast_fusion.2 = f32[2,2,4,256,256]{3,4,1,0,2:T(8,128)S(1)} fusion(bf16[1,2,256,128]{3,2,1,0:T(8,128)(2,1)} %get-tuple-element.28, bf16[1,2,256,128]{3,2,1,0:T(8,128)(2,1)} %get-tuple-element.27, bf16[4,128,256]{2,1,0:T(8,128)(2,1)} %reshape_reshape.3), kind=kOutput, calls=%fused_computation.5 | convolution fusion | flops 268959744 | bytes 4718592 | tf_op jit(solution)/shard_map/hzkn,cnm->hzckm/dot_general | solution.py:42
  72.7 0.0 copy-done.4
  72.7 0.0 copy-done.5
  72.7 0.0 copy-start.6
  72.7 0.0 copy-start.7
  72.7 0.3 multiply_add_fusion.2
  73.1 0.6 copy-done.6
  73.7 0.1 copy-done.7
  73.8 2.0 %convolution_bitcast_fusion.1 = f32[2,2,4,256,256]{3,4,2,0,1:T(8,128)S(1)} fusion(f32[1,4,256,256]{2,3,1,0:T(8,128)S(1)} %get-tuple-element.14, f32[1,4,256,256]{2,3,1,0:T(8,128)S(1)} %get-tuple-element.13, f32[1,256,256]{2,1,0:T(8,128)S(1)} %copy-done.7, f32[1,256,256]{2,1,0:T(8,128)S(1)} %copy-done.6), kind=kOutput, calls=%fused_computation.4 | convolution fusion | flops 1611268096 | bytes 6815744 | tf_op jit(solution)/shard_map/zckn,wnj->zwckj/dot_general | solution.py:10
  75.8 0.0 copy-done.2
  75.8 0.4 multiply_subtract_fusion.1
  76.2 1.9 %convolution_bitcast_fusion = f32[2,2,4,256,256]{3,4,2,1,0:T(8,128)S(1)} fusion(f32[1,4,256,256]{2,3,1,0:T(8,128)S(1)} %get-tuple-element.10, f32[1,4,256,256]{2,3,1,0:T(8,128)S(1)} %get-tuple-element.9, f32[1,256,256]{2,1,0:T(8,128)S(1)} %copy-done.7, f32[1,256,256]{2,1,0:T(8,128)S(1)} %copy-done.6), kind=kOutput, calls=%fused_computation.3 | convolution fusion | flops 1611268096 | bytes 6815744 | tf_op jit(solution)/shard_map/zckj,wjn->zwckn/dot_general | solution.py:10
  78.1 0.0 copy-start.8
  78.1 0.3 multiply_subtract_fusion
  78.5 0.6 copy-done.8
  79.0 1.0 fusion.24
  80.0 0.2 copy.112
  80.2 0.1 mul.280
  80.4 0.1 fusion.50
  80.5 0.2 copy.113
  80.7 19.6 %all_to_all.10 = bf16[32,4,1024]{2,1,0:T(4,128)(2,1)S(1)} all-to-all(bf16[32,4,1024]{2,1,0:T(4,128)(2,1)S(1)} %copy.113), channel_id=1, replica_groups=mesh['seq'=32,'chan'=16] {'seq'}, dimensions={0} | all-to-all | bytes 524288 | tf_op jit(solution)/shard_map/all_to_all | solution.py:89
  100.4 0.8 reshape.433
  (3 shorter events, 0.0 us)
Async XLA Ops:
  0.0 1.2 %copy-start = (bf16[2,128,2,1024]{3,2,1,0:T(2,128)(2,1)S(1)}, bf16[2,128,2,1024]{3,2,1,0:T(2,128)(2,1)}, u32[]{:S(2)}) copy-start(bf16[2,128,2,1024]{3,2,1,0:T(2,128)(2,1)} %param.4) | copy-start | bytes 3145732
  2.6 1.1 %copy-start.9 = (bf16[128,1024]{1,0:T(8,128)(2,1)S(1)}, bf16[128,1024]{1,0:T(8,128)(2,1)}, u32[]{:S(2)}) copy-start(bf16[128,1024]{1,0:T(8,128)(2,1)} %param.3) | copy-start | bytes 786436
  3.7 17.0 %copy-start.10 = (s32[256]{0:T(256)S(1)}, s32[256]{0:T(256)}, u32[]{:S(2)}) copy-start(s32[256]{0:T(256)} %constant.91.clone.1) | copy-start | bytes 3076
  5.7 54.8 %all-to-all-start = ((bf16[32,4,5,1024]{3,1,2,0:T(4,128)(2,1)}), bf16[32,4,5,1024]{3,1,2,0:T(4,128)(2,1)S(1)}, u32[]{:S(2)}, u32[]{:S(2)}) async-start(bf16[32,4,5,1024]{3,1,2,0:T(4,128)(2,1)} %pad_maximum_fusion), calls=%async_computation | async-start | bytes 2621440 | tf_op jit(solution)/shard_map/all_to_all | solution.py:82
  24.0 0.9 copy-start.3
  24.0 4.0 %copy-start.11 = (f32[128]{0:T(128)S(1)}, f32[128]{0:T(128)}, u32[]{:S(2)}) copy-start(f32[128]{0:T(128)} %param.5) | copy-start | bytes 1540
  67.7 2.1 %copy-start.1 = (f32[1,4,32,2,4,256]{5,4,2,3,0,1:T(4,128)S(1)}, f32[1,4,32,2,4,256]{5,4,2,3,0,1:T(4,128)}, u32[]{:S(2)}) copy-start(f32[1,4,32,2,4,256]{5,4,2,3,0,1:T(4,128)} %get-tuple-element.15) | copy-start | bytes 3145732
  70.8 1.9 %copy-start.4 = (f32[256,256]{0,1:T(8,128)S(1)}, f32[256,256]{0,1:T(8,128)}, u32[]{:S(2)}) copy-start(f32[256,256]{0,1:T(8,128)} %copy.96) | copy-start | bytes 786436
  70.9 1.9 %copy-start.5 = (f32[256,256]{0,1:T(8,128)S(1)}, f32[256,256]{0,1:T(8,128)}, u32[]{:S(2)}) copy-start(f32[256,256]{0,1:T(8,128)} %copy.97) | copy-start | bytes 786436
  72.7 1.0 copy-start.6
  72.7 1.0 %copy-start.7 = (f32[1,256,256]{2,1,0:T(8,128)S(1)}, f32[1,256,256]{2,1,0:T(8,128)}, u32[]{:S(2)}) copy-start(f32[1,256,256]{2,1,0:T(8,128)} %get-tuple-element.23) | copy-start | bytes 786436
  73.8 2.0 %copy-start.2 = (f32[1,4,256,256]{2,3,1,0:T(8,128)S(1)}, f32[1,4,256,256]{2,3,1,0:T(8,128)}, u32[]{:S(2)}) copy-start(f32[1,4,256,256]{2,3,1,0:T(8,128)} %copy.104) | copy-start | bytes 3145732
  78.1 0.9 copy-start.8

commit v3 on v2

--- a/solution.py
+++ b/solution.py
@@ -75,14 +75,15 @@
     perm = cols[:, None] == (cols[None, :] % n2_len) * rep + cols[None, :] // n2_len
     spc = jnp.einsum("rcab,bq->rcaq", spectrum, perm.astype(jnp.bfloat16),
                      preferred_element_type=jnp.float32).astype(jnp.bfloat16)
-    spc = spc.reshape(2, parts, cpd, a_loc, nb).transpose(1, 2, 0, 3, 4)
-    spc = spc.reshape(parts, cpd, 2 * a_loc, nb)
-    sig = signal.reshape(parts, cpd, 1, slab)
-    buf = jnp.concatenate([sig, spc], axis=2)
+    spc = spc.reshape(2, parts, cpd, a_loc * rep, n2_len).transpose(1, 2, 0, 3, 4)
+    spc = spc.reshape(parts, cpd, 2 * a_loc * rep, n2_len)
+    sig = signal.reshape(parts, cpd, slab // n2_len, n2_len)
+    buf = jnp.concatenate([spc, sig], axis=2)
     got = lax.all_to_all(buf, "seq", 0, 0, tiled=True)
-    x = got[:, :, 0].transpose(1, 0, 2).reshape(cpd, parts * slab)
-    s = got[:, :, 1:].reshape(parts, cpd, 2, a_loc, rep, n2_len).astype(jnp.float32)
-    s = s.transpose(2, 1, 0, 3, 4, 5).reshape(2, cpd, n1_len, n2_len)
+    spec_rows = 2 * a_loc * rep
+    x = got[:, :, spec_rows:].transpose(1, 0, 2, 3).reshape(cpd, parts * slab)
+    s = got[:, :, :spec_rows].reshape(parts, cpd, 2, a_loc * rep, n2_len).astype(jnp.float32)
+    s = s.transpose(2, 1, 0, 3, 4).reshape(2, cpd, n1_len, n2_len)
     gain = lax.dynamic_slice_in_dim(skip_gain, seq_rank * cpd, cpd)
     out = local_conv(x, s, gain, n1_len, km)
     back = out.reshape(cpd, parts, slab).transpose(1, 0, 2)

time: 101 us -> 96.9 us (0.959)
  other arithmetic: 9.63 us -> 7.22 us
  waiting for transfers between devices: 30 us -> 28.4 us
    slice x3 -> x1, local copies, waits for them, and re-layouts: 2.69 us -> 0.3 us  [local_conv(): pr = xfr * s[0] - xfi * s[1]]
    transpose x2 -> x1, local copies, waits for them, and re-layouts: 2.98 us -> 0.91 us  [per_device(): x = got[:, :, spec_rows:].transpose(1, 0, 2, 3).reshape(cpd, parts * slab)]
    concatenate x1, other arithmetic: 1.91 us -> 0.22 us  [per_device(): buf = jnp.concatenate([spc, sig], axis=2)]
    transpose x1, other arithmetic: 1.95 us -> 0.29 us  [per_device(): s = s.transpose(2, 1, 0, 3, 4).reshape(2, cpd, n1_len, n2_len)]
    all_to_all x1, waiting for transfers between devices: 30 us -> 28.4 us  [per_device(): got = lax.all_to_all(buf, 'seq', 0, 0, tiled=True)]
    concatenate x0 -> x1, local copies, waits for them, and re-layouts: none -> 1.57 us  [per_device(): buf = jnp.concatenate([spc, sig], axis=2)]
    slice x2, local copies, waits for them, and re-layouts: 1.68 us -> 2.86 us  [local_conv(): tc, ts = (tab_c[n1_len + n2_len:], tab_s[n1_len + n2_len:])]
    convert_element_type x0 -> x2, local copies, waits for them, and re-layouts: none -> 1.04 us  [the longest x1 1 us: per_device(): spc = jnp.einsum('rcab,bq->rcaq', spectrum, perm.astype(jnp.bfloat16), pr...]
  transfers between devices with their start and end apart: 1 -> 1, of which waited for: 1 -> 1; matrix products, arithmetic and copies ran while one was open for 9% -> 11% of each run, Pallas kernels for 0% -> 0%
where the time goes in v3:
time: 96.9 us; the launch traced here: 96.5 us
  waiting for transfers between devices  28.4 us (29%)
  blocking collectives  19.6 us (20%)
  local copies, waits for them, and re-layouts  17.6 us (18%)
  starting transfers between devices  15.2 us (16%)
  matrix products  8.02 us (8%)
  other arithmetic  7.22 us (7%)
    all_to_all x1, waiting for transfers between devices, per_device(): got = lax.all_to_all(buf, 'seq', 0, 0, tiled=True)  28.4 us
    all_to_all x1, blocking collectives, per_device(): back = lax.all_to_all(back, 'seq', 0, 0, tiled=True)  19.6 us
    all_to_all x1, starting transfers between devices, per_device(): got = lax.all_to_all(buf, 'seq', 0, 0, tiled=True)  15.2 us
    dot_general x3, matrix products, dot_hi(): jnp.einsum(form, left, right, precision=lax.Precision.HIGH, preferred_ele...  4.91 us
    unnamed x22, local copies, waits for them, and re-layouts  3.79 us
    slice x2, local copies, waits for them, and re-layouts, local_conv(): tc, ts = (tab_c[n1_len + n2_len:], tab_s[n1_len + n2_len:])  2.86 us
    sin x1, other arithmetic, local_conv(): tab_c, tab_s = lax.optimization_barrier((jnp.cos(angles), jnp.sin(angles)))  2.75 us
  transfers between devices with their start and end apart: 1, of which 1 were waited for; matrix products, arithmetic and copies ran while one was open for 11% of the time, Pallas kernels for 0%

profile of v3, /device:TPU:14, one launch (start us, length us, event | category | flops | bytes accessed | tf_op | source)
XLA Modules:
  0.0 96.5 jit_solution(9227767347582593060)
XLA Ops:
  0.0 0.0 copy-start
  0.0 1.2 %copy-done = bf16[2,128,2,1024]{3,2,1,0:T(2,128)(2,1)S(1)} copy-done((bf16[2,128,2,1024]{3,2,1,0:T(2,128)(2,1)S(1)}, bf16[2,128,2,1024]{3,2,1,0:T(2,128)(2,1)}, u32[]{:S(2)}) %copy-start) | copy-done | bytes 1048600
  1.2 1.3 %fusion.15 = bf16[2,128,2,1024]{1,3,2,0:T(8,128)(2,1)S(1)} fusion(s32[1024]{0:T(1024)S(1)} %fusion.70, bf16[2,128,2,1024]{3,2,1,0:T(2,128)(2,1)S(1)} %copy-done), kind=kOutput, calls=%fused_computation.20 | convolution fusion | flops 1075314688 | bytes 2101248 | tf_op jit(solution)/shard_map/rcab,bq->rcaq/dot_general | solution.py:76
  2.5 1.0 %copy.96 = bf16[2,128,2,1024]{3,2,1,0:T(2,128)(2,1)S(1)} copy(bf16[2,128,2,1024]{1,3,2,0:T(8,128)(2,1)S(1)} %fusion.15) | data formatting | bytes 2097152 | tf_op jit(solution)/shard_map/convert_element_type | solution.py:77
  3.5 0.0 copy-start.8
  3.5 0.4 reshape.433
  4.0 0.1 copy_bitcast_fusion.3
  4.1 0.4 copy-done.8
  4.5 0.2 reshape.435
  4.7 0.2 pad_maximum_fusion
  4.9 0.0 copy-start.9
  4.9 1.6 %copy.98 = bf16[32,4,20,256]{3,1,2,0:T(4,128)(2,1)} copy(bf16[32,4,20,256]{3,2,1,0:T(8,128)(2,1)S(1)} %pad_maximum_fusion) | data formatting | bytes 2621440 | tf_op jit(solution)/shard_map/concatenate | solution.py:81
  6.5 15.2 %all-to-all-start = ((bf16[32,4,20,256]{3,1,2,0:T(4,128)(2,1)}), bf16[32,4,20,256]{3,1,2,0:T(4,128)(2,1)S(1)}, u32[]{:S(2)}, u32[]{:S(2)}) async-start(bf16[32,4,20,256]{3,1,2,0:T(4,128)(2,1)} %copy.98), calls=%async_computation | async-start | bytes 2621440 | tf_op jit(solution)/shard_map/all_to_all | solution.py:82
  21.8 0.0 copy-done.9
  21.8 0.4 fusion.42
  22.2 2.8 %fusion.36 = (f32[768,256]{1,0:T(8,128)S(1)}, f32[768,256]{1,0:T(8,128)S(1)}) fusion(f32[256,256]{1,0:T(8,128)S(1)} %get-tuple-element.32, f32[256,256]{1,0:T(8,128)S(1)} %get-tuple-element.33, f32[256,256]{1,0:T(8,128)S(1)} %get-tuple-element.31), kind=kLoop, calls=%fused_computation.52 | loop fusion | flops 393216 | bytes 2359296 | tf_op jit(solution)/shard_map/sin | solution.py:33
  25.0 0.0 copy-start.2
  25.0 0.0 copy-start.10
  25.0 0.9 copy-done.2
  25.8 0.8 slice_bitcast_fusion.5
  26.7 1.1 %copy.104 = f32[256,256]{0,1:T(8,128)S(1)} copy(f32[256,256]{1,0:T(8,128)} %get-tuple-element.22) | data formatting | bytes 524288 | tf_op jit(solution)/shard_map/slice | solution.py:36
  27.8 0.8 slice_bitcast_fusion.4
  28.6 1.8 %copy.105 = f32[256,256]{0,1:T(8,128)} copy(f32[256,256]{1,0:T(8,128)} %get-tuple-element.24) | data formatting | bytes 524288 | tf_op jit(solution)/shard_map/slice | solution.py:36
  30.4 0.0 copy-done.10
  30.4 0.1 dynamic_slice.3
  30.5 0.9 slice_bitcast_fusion.6
  31.4 0.7 fusion.62
  32.1 0.8 reduce-precision_convert_fusion
  32.8 28.4 %all-to-all-done = bf16[32,4,20,256]{3,1,2,0:T(4,128)(2,1)S(1)} async-done(((bf16[32,4,20,256]{3,1,2,0:T(4,128)(2,1)}), bf16[32,4,20,256]{3,1,2,0:T(4,128)(2,1)S(1)}, u32[]{:S(2)}, u32[]{:S(2)}) %all-to-all-start) | async-done | bytes 1310752 | tf_op jit(solution)/shard_map/all_to_all | solution.py:82
  61.2 0.1 slice.92
  61.3 0.9 convert_bitcast_fusion.1
  62.2 0.9 copy.100
  63.2 0.5 slice.99
  63.7 0.3 convert_bitcast_fusion
  64.0 0.3 fusion.81
  64.3 0.2 copy_bitcast_fusion.1
  64.5 1.3 %copy.112 = f32[1,4,256,256]{2,3,1,0:T(8,128)} copy(f32[1,4,256,256]{3,2,1,0:T(8,128)S(1)} %get-tuple-element.35) | data formatting | bytes 2097152 | tf_op jit(solution)/shard_map/squeeze | solution.py:51
  65.9 0.3 copy.114
  66.2 0.0 copy-start.3
  66.2 1.8 %convolution_bitcast_fusion.2 = f32[2,2,4,256,256]{3,4,1,0,2:T(8,128)S(1)} fusion(bf16[1,2,256,128]{3,2,1,0:T(8,128)(2,1)} %get-tuple-element.30, bf16[1,2,256,128]{3,2,1,0:T(8,128)(2,1)} %get-tuple-element.29, bf16[4,128,256,1,1]{2,0,1,4,3:T(4,128)(2,1)} %bitcast.164), kind=kOutput, calls=%fused_computation.5 | convolution fusion | flops 268959744 | bytes 4718592 | tf_op jit(solution)/shard_map/hzkn,cnm->hzckm/dot_general | solution.py:42
  68.0 0.0 copy-done.3
  68.0 0.0 copy-start.4
  68.0 0.0 copy-start.5
  68.1 0.3 multiply_add_fusion.2
  68.4 0.6 copy-done.4
  69.0 0.1 copy-done.5
  69.1 0.0 copy-start.1
  69.1 2.0 %convolution_bitcast_fusion.1 = f32[2,2,4,256,256]{3,4,2,0,1:T(8,128)S(1)} fusion(f32[1,4,256,256]{2,3,1,0:T(8,128)S(1)} %get-tuple-element.14, f32[1,4,256,256]{2,3,1,0:T(8,128)S(1)} %get-tuple-element.13, f32[1,256,256]{2,1,0:T(8,128)S(1)} %copy-done.5, f32[1,256,256]{2,1,0:T(8,128)S(1)} %copy-done.4), kind=kOutput, calls=%fused_computation.4 | convolution fusion | flops 1611268096 | bytes 6815744 | tf_op jit(solution)/shard_map/zckn,wnj->zwckj/dot_general | solution.py:10
  71.1 0.0 copy-done.1
  71.1 0.4 multiply_subtract_fusion.1
  71.5 1.9 %convolution_bitcast_fusion = f32[2,2,4,256,256]{3,4,2,1,0:T(8,128)S(1)} fusion(f32[1,4,256,256]{2,3,1,0:T(8,128)S(1)} %get-tuple-element.10, f32[1,4,256,256]{2,3,1,0:T(8,128)S(1)} %get-tuple-element.9, f32[1,256,256]{2,1,0:T(8,128)S(1)} %copy-done.5, f32[1,256,256]{2,1,0:T(8,128)S(1)} %copy-done.4), kind=kOutput, calls=%fused_computation.3 | convolution fusion | flops 1611268096 | bytes 6815744 | tf_op jit(solution)/shard_map/zckj,wjn->zwckn/dot_general | solution.py:10
  73.4 0.0 copy-start.7
  73.4 0.3 multiply_subtract_fusion
  73.8 0.6 copy-done.7
  74.3 0.0 copy-start.6
  74.3 1.0 %fusion.24 = f32[4,128,256]{1,2,0:T(8,128)S(1)} fusion(f32[1,4,256,256]{2,3,1,0:T(8,128)S(1)} %get-tuple-element.12, f32[1,4,256,256]{2,3,1,0:T(8,128)S(1)} %get-tuple-element.11, f32[1,256,128]{2,1,0:T(8,128)S(1)} %copy-done.7, f32[1,256,128]{2,1,0:T(8,128)S(1)} %get-tuple-element.17), kind=kOutput, calls=%fused_computation.23 | convolution fusion | flops 403374080 | bytes 2883584 | tf_op jit(solution)/shard_map/zkn,zckm->cnm/dot_general | solution.py:10
  75.3 0.2 copy.120
  75.5 0.1 mul.280
  75.7 0.0 copy-done.6
  75.8 0.1 fusion.50
  75.9 0.2 copy.122
  76.1 19.6 %all_to_all.10 = bf16[32,4,1024]{2,1,0:T(4,128)(2,1)S(1)} all-to-all(bf16[32,4,1024]{2,1,0:T(4,128)(2,1)S(1)} %copy.122), channel_id=1, replica_groups=mesh['seq'=32,'chan'=16] {'seq'}, dimensions={0} | all-to-all | bytes 524288 | tf_op jit(solution)/shard_map/all_to_all | solution.py:90
  95.7 0.8 reshape.436
  (3 shorter events, 0.1 us)
Async XLA Ops:
  0.0 1.2 %copy-start = (bf16[2,128,2,1024]{3,2,1,0:T(2,128)(2,1)S(1)}, bf16[2,128,2,1024]{3,2,1,0:T(2,128)(2,1)}, u32[]{:S(2)}) copy-start(bf16[2,128,2,1024]{3,2,1,0:T(2,128)(2,1)} %param.4) | copy-start | bytes 3145732
  3.5 1.0 copy-start.8
  4.9 16.9 %copy-start.9 = (s32[256]{0:T(256)S(1)}, s32[256]{0:T(256)}, u32[]{:S(2)}) copy-start(s32[256]{0:T(256)} %constant.91.clone.1) | copy-start | bytes 3076
  6.5 54.8 %all-to-all-start = ((bf16[32,4,20,256]{3,1,2,0:T(4,128)(2,1)}), bf16[32,4,20,256]{3,1,2,0:T(4,128)(2,1)S(1)}, u32[]{:S(2)}, u32[]{:S(2)}) async-start(bf16[32,4,20,256]{3,1,2,0:T(4,128)(2,1)} %copy.98), calls=%async_computation | async-start | bytes 2621440 | tf_op jit(solution)/shard_map/all_to_all | solution.py:82
  25.0 0.9 copy-start.2
  25.0 5.4 %copy-start.10 = (f32[128]{0:T(128)S(1)}, f32[128]{0:T(128)}, u32[]{:S(2)}) copy-start(f32[128]{0:T(128)} %param.5) | copy-start | bytes 1540
  66.2 1.8 %copy-start.3 = (f32[256,256]{0,1:T(8,128)S(1)}, f32[256,256]{0,1:T(8,128)}, u32[]{:S(2)}) copy-start(f32[256,256]{0,1:T(8,128)} %copy.105) | copy-start | bytes 786436
  68.0 1.0 copy-start.4
  68.0 1.0 %copy-start.5 = (f32[1,256,256]{2,1,0:T(8,128)S(1)}, f32[1,256,256]{2,1,0:T(8,128)}, u32[]{:S(2)}) copy-start(f32[1,256,256]{2,1,0:T(8,128)} %get-tuple-element.23) | copy-start | bytes 786436
  69.1 2.0 %copy-start.1 = (f32[1,4,256,256]{2,3,1,0:T(8,128)S(1)}, f32[1,4,256,256]{2,3,1,0:T(8,128)}, u32[]{:S(2)}) copy-start(f32[1,4,256,256]{2,3,1,0:T(8,128)} %copy.112) | copy-start | bytes 3145732
  73.4 0.9 copy-start.7
  74.3 1.4 %copy-start.6 = (f32[4,4,4,8,256]{4,3,2,1,0:T(8,128)S(1)}, f32[4,4,4,8,256]{4,3,2,1,0:T(8,128)}, u32[]{:S(2)}) copy-start(f32[4,4,4,8,256]{4,3,2,1,0:T(8,128)} %get-tuple-element.27) | copy-start | bytes 1572868

commit v4 on v3

--- a/solution.py
+++ b/solution.py
@@ -16,9 +16,10 @@
 
 
 def local_conv(x, s, gain, n1_len, km):
-    count, length = x.shape
+    n2_len = s.shape[3]
+    parts, count = x.shape[0], x.shape[1]
+    length = parts * x.shape[2] * x.shape[3]
     full_len = 2 * length
-    n2_len = full_len // n1_len
     half1 = length // n2_len
     rep = n1_len // km
     rows = jnp.arange(n1_len, dtype=jnp.int32)
@@ -34,13 +35,13 @@
     f1c, f1s = tab_c[:n1_len, :half1], tab_s[:n1_len, :half1]
     wc, ws = tab_c[n1_len:n1_len + n2_len], tab_s[n1_len:n1_len + n2_len]
     tc, ts = tab_c[n1_len + n2_len:], tab_s[n1_len + n2_len:]
-    xr = x.reshape(count, half1, n2_len)
+    xr = x
     f1 = jnp.stack([f1c, -f1s])
     f1_top = lax.reduce_precision(f1, exponent_bits=8, mantissa_bits=7)
     f1_hi = f1_top.astype(jnp.bfloat16)
     f1_lo = (f1 - f1_top).astype(jnp.bfloat16)
-    a = jnp.einsum("hzkn,cnm->hzckm", jnp.stack([f1_hi, f1_lo]), xr,
-                   preferred_element_type=jnp.float32)
+    f1_hl = jnp.stack([f1_hi, f1_lo]).reshape(2, 2, n1_len, parts, half1 // parts)
+    a = jnp.einsum("hzkpi,pcim->hzckm", f1_hl, xr, preferred_element_type=jnp.float32)
     ar, ai = a[0, 0] + a[1, 0], a[0, 1] + a[1, 1]
     br = ar * tc + ai * ts
     bi = ai * tc - ar * ts
@@ -57,7 +58,8 @@
     ri = qi * tc + qr * ts
     y = dot_hi("zkn,zckm->cnm", jnp.stack([f1c, -f1s]), jnp.stack([rr, ri]))
     y = y.reshape(count, length) * (1.0 / full_len)
-    return (y + gain[:, None] * x.astype(jnp.float32)).astype(jnp.bfloat16)
+    xs = x.transpose(1, 0, 2, 3).reshape(count, length).astype(jnp.float32)
+    return (y + gain[:, None] * xs).astype(jnp.bfloat16)
 
 
 def per_device(signal, spectrum, skip_gain):
@@ -81,7 +83,7 @@
     buf = jnp.concatenate([spc, sig], axis=2)
     got = lax.all_to_all(buf, "seq", 0, 0, tiled=True)
     spec_rows = 2 * a_loc * rep
-    x = got[:, :, spec_rows:].transpose(1, 0, 2, 3).reshape(cpd, parts * slab)
+    x = got[:, :, spec_rows:]
     s = got[:, :, :spec_rows].reshape(parts, cpd, 2, a_loc * rep, n2_len).astype(jnp.float32)
     s = s.transpose(2, 1, 0, 3, 4).reshape(2, cpd, n1_len, n2_len)
     gain = lax.dynamic_slice_in_dim(skip_gain, seq_rank * cpd, cpd)

time: 96.9 us -> 98.2 us (1.013)
  local copies, waits for them, and re-layouts: 17.6 us -> 18.9 us
  waiting for transfers between devices: 28.4 us -> 29.4 us
    squeeze x3, local copies, waits for them, and re-layouts: 1.86 us -> 5.03 us  [local_conv(): pr = xfr * s[0] - xfi * s[1]]
    slice x3 -> x1, local copies, waits for them, and re-layouts: 2.96 us -> 0.09 us  [per_device(): x = got[:, :, spec_rows:]]
    another operation x2, local copies, waits for them, and re-layouts: 1.66 us -> 2.7 us  [local_conv(): w = jnp.stack([wc, ws])]
    all_to_all x1, waiting for transfers between devices: 28.4 us -> 29.4 us  [per_device(): got = lax.all_to_all(buf, 'seq', 0, 0, tiled=True)]
    unnamed x22 -> x25, local copies, waits for them, and re-layouts: 3.79 us -> 3.83 us
  transfers between devices with their start and end apart: 1 -> 1, of which waited for: 1 -> 1; matrix products, arithmetic and copies ran while one was open for 11% -> 9% of each run, Pallas kernels for 0% -> 0%
where the time goes in v4:
time: 98.2 us; the launch traced here: 97.8 us
  waiting for transfers between devices  29.4 us (30%)
  blocking collectives  19.6 us (20%)
  local copies, waits for them, and re-layouts  18.9 us (19%)
  starting transfers between devices  15.2 us (15%)
  matrix products  7.85 us (8%)
  other arithmetic  6.43 us (7%)
    all_to_all x1, waiting for transfers between devices, per_device(): got = lax.all_to_all(buf, 'seq', 0, 0, tiled=True)  29.4 us
    all_to_all x1, blocking collectives, per_device(): back = lax.all_to_all(back, 'seq', 0, 0, tiled=True)  19.6 us
    all_to_all x1, starting transfers between devices, per_device(): got = lax.all_to_all(buf, 'seq', 0, 0, tiled=True)  15.2 us
    squeeze x3, local copies, waits for them, and re-layouts, local_conv(): pr = xfr * s[0] - xfi * s[1]  5.03 us
    dot_general x3, matrix products, dot_hi(): jnp.einsum(form, left, right, precision=lax.Precision.HIGH, preferred_ele...  4.79 us
    unnamed x25, local copies, waits for them, and re-layouts  3.83 us
    sin x1, other arithmetic, local_conv(): tab_c, tab_s = lax.optimization_barrier((jnp.cos(angles), jnp.sin(angles)))  2.8 us
    another operation x2, local copies, waits for them, and re-layouts, local_conv(): w = jnp.stack([wc, ws])  2.7 us
  transfers between devices with their start and end apart: 1, of which 1 were waited for; matrix products, arithmetic and copies ran while one was open for 9% of the time, Pallas kernels for 0%

profile of v4, /device:TPU:14, one launch (start us, length us, event | category | flops | bytes accessed | tf_op | source)
XLA Modules:
  0.0 97.8 jit_solution(1503354681407119273)
XLA Ops:
  0.0 0.0 copy-start
  0.0 1.2 %copy-done = bf16[2,128,2,1024]{3,2,1,0:T(2,128)(2,1)S(1)} copy-done((bf16[2,128,2,1024]{3,2,1,0:T(2,128)(2,1)S(1)}, bf16[2,128,2,1024]{3,2,1,0:T(2,128)(2,1)}, u32[]{:S(2)}) %copy-start) | copy-done | bytes 1048600
  1.2 1.3 %fusion.15 = bf16[2,128,2,1024]{1,3,2,0:T(8,128)(2,1)S(1)} fusion(s32[1024]{0:T(1024)S(1)} %fusion.69, bf16[2,128,2,1024]{3,2,1,0:T(2,128)(2,1)S(1)} %copy-done), kind=kOutput, calls=%fused_computation.20 | convolution fusion | flops 1075314688 | bytes 2101248 | tf_op jit(solution)/shard_map/rcab,bq->rcaq/dot_general | solution.py:78
  2.5 1.0 %copy.105 = bf16[2,128,2,1024]{3,2,1,0:T(2,128)(2,1)S(1)} copy(bf16[2,128,2,1024]{1,3,2,0:T(8,128)(2,1)S(1)} %fusion.15) | data formatting | bytes 2097152 | tf_op jit(solution)/shard_map/convert_element_type | solution.py:79
  3.5 0.0 copy-start.9
  3.5 0.4 reshape.444
  4.0 0.1 copy_bitcast_fusion.3
  4.1 0.4 copy-done.9
  4.5 0.2 reshape.446
  4.7 0.2 pad_maximum_fusion
  4.9 0.0 copy-start.10
  4.9 1.6 %copy.107 = bf16[32,4,20,256]{3,1,2,0:T(4,128)(2,1)} copy(bf16[32,4,20,256]{3,2,1,0:T(8,128)(2,1)S(1)} %pad_maximum_fusion) | data formatting | bytes 2621440 | tf_op jit(solution)/shard_map/concatenate | solution.py:83
  6.5 15.2 %all-to-all-start = ((bf16[32,4,20,256]{3,1,2,0:T(4,128)(2,1)}), bf16[32,4,20,256]{3,1,2,0:T(4,128)(2,1)S(1)}, u32[]{:S(2)}, u32[]{:S(2)}) async-start(bf16[32,4,20,256]{3,1,2,0:T(4,128)(2,1)} %copy.107), calls=%async_computation | async-start | bytes 2621440 | tf_op jit(solution)/shard_map/all_to_all | solution.py:84
  21.8 0.0 copy-done.10
  21.8 0.0 copy-start.11
  21.8 0.4 fusion.42
  22.2 2.8 %fusion.36 = (f32[768,256]{0,1:T(8,128)S(1)}, f32[768,256]{0,1:T(8,128)S(1)}) fusion(f32[256,256]{0,1:T(8,128)S(1)} %get-tuple-element.30, f32[256,256]{0,1:T(8,128)S(1)} %get-tuple-element.31, f32[256,256]{0,1:T(8,128)S(1)} %get-tuple-element.29), kind=kLoop, calls=%fused_computation.52 | loop fusion | flops 393216 | bytes 2359296 | tf_op jit(solution)/shard_map/sin | solution.py:34
  25.0 0.0 copy-start.3
  25.0 0.9 copy-done.3
  26.0 0.7 fusion.80
  26.6 0.7 stack.51
  27.3 0.0 copy-done.11
  27.3 0.1 dynamic_slice.3
  27.4 0.9 copy_dynamic-update-slice_fusion
  28.4 1.9 %slice_bitcast_fusion.5 = (f32[1,256,256]{1,2,0:T(8,128)}, f32[256,256]{0,1:T(8,128)}) fusion(f32[768,256]{0,1:T(8,128)} %copy-done.3), kind=kLoop, calls=%fused_computation.91 | loop fusion | bytes 1048576 | tf_op jit(solution)/shard_map/stack | solution.py:48
  30.2 0.8 slice_bitcast_fusion.4
  31.1 0.7 reduce-precision_convert_fusion
  31.8 29.4 %all-to-all-done = bf16[32,4,20,256]{3,1,2,0:T(4,128)(2,1)S(1)} async-done(((bf16[32,4,20,256]{3,1,2,0:T(4,128)(2,1)}), bf16[32,4,20,256]{3,1,2,0:T(4,128)(2,1)S(1)}, u32[]{:S(2)}, u32[]{:S(2)}) %all-to-all-start) | async-done | bytes 1310752 | tf_op jit(solution)/shard_map/all_to_all | solution.py:84
  61.2 0.5 slice.99
  61.8 0.3 convert_bitcast_fusion
  62.1 0.3 fusion.81
  62.4 1.2 %copy_bitcast_fusion.1 = (f32[1,4,256,256]{3,2,1,0:T(8,128)S(1)}, f32[1,4,256,256]{3,2,1,0:T(8,128)}) fusion(f32[1,4,32,8,256]{4,3,0,1,2:T(8,128)S(1)} %get-tuple-element.15, f32[1,4,32,8,256]{4,3,0,1,2:T(8,128)S(1)} %get-tuple-element.16), kind=kLoop, calls=%fused_computation.41 | loop fusion | bytes 4194304 | tf_op jit(solution)/shard_map/squeeze | solution.py:52
  63.6 2.6 %copy.118 = f32[1,4,256,256]{2,3,1,0:T(8,128)} copy(f32[1,4,256,256]{3,2,1,0:T(8,128)} %get-tuple-element.33) | data formatting | bytes 2097152 | tf_op jit(solution)/shard_map/squeeze | solution.py:52
  66.1 1.3 %copy.120 = f32[1,4,256,256]{2,3,1,0:T(8,128)} copy(f32[1,4,256,256]{3,2,1,0:T(8,128)S(1)} %get-tuple-element.32) | data formatting | bytes 2097152 | tf_op jit(solution)/shard_map/squeeze | solution.py:52
  67.4 0.1 slice.92
  67.5 0.1 convert_bitcast_fusion.1
  67.6 0.0 copy-start.4
  67.6 0.0 copy-start.5
  67.6 1.8 %convolution_bitcast_fusion.2 = f32[2,2,4,256,256]{3,4,1,0,2:T(8,128)S(1)} fusion(bf16[1,2,256,32,4]{2,3,4,1,0:T(8,128)(2,1)} %get-tuple-element.28, bf16[1,2,256,32,4]{2,3,4,1,0:T(8,128)(2,1)} %get-tuple-element.27, bf16[32,4,4,256]{3,1,2,0:T(4,128)(2,1)S(1)} %slice.92), kind=kOutput, calls=%fused_computation.5 | convolution fusion | flops 268959744 | bytes 4718592 | tf_op jit(solution)/shard_map/hzkpi,pcim->hzckm/dot_general | solution.py:44
  69.4 0.0 copy-done.4
  69.4 0.0 copy-done.5
  69.4 0.0 copy-start.6
  69.4 0.0 copy-start.7
  69.4 0.3 multiply_add_fusion.2
  69.8 0.6 copy-done.6
  70.4 0.1 copy-done.7
  70.5 0.0 copy-start.1
  70.5 0.0 copy-start.2
  70.5 1.9 %convolution_bitcast_fusion.1 = f32[2,2,4,256,256]{3,4,2,0,1:T(8,128)S(1)} fusion(f32[1,4,256,256]{2,3,1,0:T(8,128)S(1)} %get-tuple-element.14, f32[1,4,256,256]{2,3,1,0:T(8,128)S(1)} %get-tuple-element.13, f32[1,256,256]{1,2,0:T(8,128)S(1)} %copy-done.7, f32[1,256,256]{1,2,0:T(8,128)S(1)} %copy-done.6), kind=kOutput, calls=%fused_computation.4 | convolution fusion | flops 1611268096 | bytes 6815744 | tf_op jit(solution)/shard_map/zckn,wnj->zwckj/dot_general | solution.py:10
  72.4 0.0 copy-done.1
  72.4 0.0 copy-done.2
  72.4 0.4 multiply_subtract_fusion.1
  72.8 1.9 %convolution_bitcast_fusion = f32[2,2,4,256,256]{3,4,2,1,0:T(8,128)S(1)} fusion(f32[1,4,256,256]{2,3,1,0:T(8,128)S(1)} %get-tuple-element.10, f32[1,4,256,256]{2,3,1,0:T(8,128)S(1)} %get-tuple-element.9, f32[1,256,256]{1,2,0:T(8,128)S(1)} %copy-done.7, f32[1,256,256]{1,2,0:T(8,128)S(1)} %copy-done.6), kind=kOutput, calls=%fused_computation.3 | convolution fusion | flops 1611268096 | bytes 6815744 | tf_op jit(solution)/shard_map/zckj,wjn->zwckn/dot_general | solution.py:10
  74.7 0.0 copy-start.8
  74.7 0.3 multiply_subtract_fusion
  75.0 0.6 copy-done.8
  75.6 1.0 %fusion.24 = f32[4,128,256]{1,2,0:T(8,128)S(1)} fusion(f32[1,4,256,256]{2,3,1,0:T(8,128)S(1)} %get-tuple-element.12, f32[1,4,256,256]{2,3,1,0:T(8,128)S(1)} %get-tuple-element.11, f32[1,256,128]{1,2,0:T(8,128)S(1)} %copy-done.8, f32[1,256,128]{1,2,0:T(8,128)S(1)} %get-tuple-element.17), kind=kOutput, calls=%fused_computation.23 | convolution fusion | flops 403374080 | bytes 2883584 | tf_op jit(solution)/shard_map/zkn,zckm->cnm/dot_general | solution.py:10
  76.6 0.2 copy.126
  76.8 0.1 mul.280
  77.0 0.1 fusion.50
  77.2 0.2 copy.128
  77.4 19.6 %all_to_all.10 = bf16[32,4,1024]{2,1,0:T(4,128)(2,1)S(1)} all-to-all(bf16[32,4,1024]{2,1,0:T(4,128)(2,1)S(1)} %copy.128), channel_id=1, replica_groups=mesh['seq'=32,'chan'=16] {'seq'}, dimensions={0} | all-to-all | bytes 524288 | tf_op jit(solution)/shard_map/all_to_all | solution.py:92
  97.0 0.8 reshape.447
  (6 shorter events, 0.1 us)
Async XLA Ops:
  0.0 1.2 %copy-start = (bf16[2,128,2,1024]{3,2,1,0:T(2,128)(2,1)S(1)}, bf16[2,128,2,1024]{3,2,1,0:T(2,128)(2,1)}, u32[]{:S(2)}) copy-start(bf16[2,128,2,1024]{3,2,1,0:T(2,128)(2,1)} %param.4) | copy-start | bytes 3145732
  3.5 1.0 copy-start.9
  4.9 16.9 %copy-start.10 = (s32[256]{0:T(256)S(1)}, s32[256]{0:T(256)}, u32[]{:S(2)}) copy-start(s32[256]{0:T(256)} %constant.91.clone.1) | copy-start | bytes 3076
  6.5 54.8 %all-to-all-start = ((bf16[32,4,20,256]{3,1,2,0:T(4,128)(2,1)}), bf16[32,4,20,256]{3,1,2,0:T(4,128)(2,1)S(1)}, u32[]{:S(2)}, u32[]{:S(2)}) async-start(bf16[32,4,20,256]{3,1,2,0:T(4,128)(2,1)} %copy.107), calls=%async_computation | async-start | bytes 2621440 | tf_op jit(solution)/shard_map/all_to_all | solution.py:84
  21.8 5.6 %copy-start.11 = (f32[128]{0:T(128)S(1)}, f32[128]{0:T(128)}, u32[]{:S(2)}) copy-start(f32[128]{0:T(128)} %param.5) | copy-start | bytes 1540
  25.0 0.9 copy-start.3
  67.6 1.8 %copy-start.4 = (f32[256,256]{0,1:T(8,128)S(1)}, f32[256,256]{0,1:T(8,128)}, u32[]{:S(2)}) copy-start(f32[256,256]{0,1:T(8,128)} %get-tuple-element.22) | copy-start | bytes 786436
  67.6 1.8 %copy-start.5 = (f32[256,256]{0,1:T(8,128)S(1)}, f32[256,256]{0,1:T(8,128)}, u32[]{:S(2)}) copy-start(f32[256,256]{0,1:T(8,128)} %get-tuple-element.24) | copy-start | bytes 786436
  69.4 1.0 copy-start.6
  69.4 1.0 %copy-start.7 = (f32[1,256,256]{1,2,0:T(8,128)S(1)}, f32[1,256,256]{1,2,0:T(8,128)}, u32[]{:S(2)}) copy-start(f32[1,256,256]{1,2,0:T(8,128)} %get-tuple-element.23) | copy-start | bytes 786436
  70.5 2.0 %copy-start.1 = (f32[1,4,256,256]{2,3,1,0:T(8,128)S(1)}, f32[1,4,256,256]{2,3,1,0:T(8,128)}, u32[]{:S(2)}) copy-start(f32[1,4,256,256]{2,3,1,0:T(8,128)} %copy.118) | copy-start | bytes 3145732
  70.5 2.0 %copy-start.2 = (f32[1,4,256,256]{2,3,1,0:T(8,128)S(1)}, f32[1,4,256,256]{2,3,1,0:T(8,128)}, u32[]{:S(2)}) copy-start(f32[1,4,256,256]{2,3,1,0:T(8,128)} %copy.120) | copy-start | bytes 3145732
  74.7 0.9 copy-start.8

commit v5 on v3

--- a/solution.py
+++ b/solution.py
@@ -3,7 +3,9 @@
 import jax
 import jax.numpy as jnp
 from jax import lax
-from jax.sharding import PartitionSpec as P
+from jax.sharding import Mesh, PartitionSpec as P
+
+SEQ = ("yh", "z", "core")
 
 
 def dot_hi(form, left, right):
@@ -62,7 +64,7 @@
 
 def per_device(signal, spectrum, skip_gain):
     ch_blk, slab = signal.shape
-    parts = lax.axis_size("seq")
+    parts = lax.axis_size(SEQ)
     cpd = ch_blk // parts
     a_loc, nb = spectrum.shape[2], spectrum.shape[3]
     km = parts * a_loc
@@ -70,7 +72,7 @@
     n1_len = 1 << (int(math.log2(full_len)) // 2)
     n2_len = full_len // n1_len
     rep = n1_len // km
-    seq_rank = lax.axis_index("seq")
+    seq_rank = lax.axis_index(SEQ)
     cols = jnp.arange(nb, dtype=jnp.int32)
     perm = cols[:, None] == (cols[None, :] % n2_len) * rep + cols[None, :] // n2_len
     spc = jnp.einsum("rcab,bq->rcaq", spectrum, perm.astype(jnp.bfloat16),
@@ -79,7 +81,10 @@
     spc = spc.reshape(parts, cpd, 2 * a_loc * rep, n2_len)
     sig = signal.reshape(parts, cpd, slab // n2_len, n2_len)
     buf = jnp.concatenate([spc, sig], axis=2)
-    got = lax.all_to_all(buf, "seq", 0, 0, tiled=True)
+    cores = lax.axis_size("core")
+    buf = buf.reshape((parts // cores, cores) + buf.shape[1:])
+    buf = lax.all_to_all(buf, "core", 1, 1, tiled=True)
+    got = lax.all_to_all(buf, ("yh", "z"), 0, 0, tiled=True).reshape((parts,) + buf.shape[2:])
     spec_rows = 2 * a_loc * rep
     x = got[:, :, spec_rows:].transpose(1, 0, 2, 3).reshape(cpd, parts * slab)
     s = got[:, :, :spec_rows].reshape(parts, cpd, 2, a_loc * rep, n2_len).astype(jnp.float32)
@@ -87,15 +92,19 @@
     gain = lax.dynamic_slice_in_dim(skip_gain, seq_rank * cpd, cpd)
     out = local_conv(x, s, gain, n1_len, km)
     back = out.reshape(cpd, parts, slab).transpose(1, 0, 2)
-    back = lax.all_to_all(back, "seq", 0, 0, tiled=True)
+    back = lax.all_to_all(back, SEQ, 0, 0, tiled=True)
     return back.reshape(ch_blk, slab)
 
 
 def solution(mesh):
+    seq_n, chan_n = mesh.devices.shape
+    cores = 2
+    fine = Mesh(mesh.devices.reshape(2, seq_n // (2 * cores), cores, chan_n),
+                ("yh", "z", "core", "chan"))
     return jax.shard_map(
         per_device,
-        mesh=mesh,
-        in_specs=(P("chan", "seq"), P(None, "chan", "seq", None), P("chan")),
-        out_specs=P("chan", "seq"),
+        mesh=fine,
+        in_specs=(P("chan", SEQ), P(None, "chan", SEQ, None), P("chan")),
+        out_specs=P("chan", SEQ),
         check_vma=False,
     )

time: 96.9 us -> 112 us (1.16)
  the two profiles are of different devices: /device:TPU:14 before, /device:TPU:10 now
where the time goes in v5:
time: 112 us; the launch traced here: 111 us
  blocking collectives  30.5 us (27%)
  waiting for transfers between devices  29.3 us (26%)
  local copies, waits for them, and re-layouts  20.6 us (18%)
  starting transfers between devices  14.8 us (13%)
  matrix products  8.02 us (7%)
  other arithmetic  7.71 us (7%)
    all_to_all x1, waiting for transfers between devices, per_device(): lax.all_to_all(buf, ('yh', 'z'), 0, 0, tiled=True)  29.3 us
    all_to_all x1, blocking collectives, per_device(): back = lax.all_to_all(back, SEQ, 0, 0, tiled=True)  25.7 us
    all_to_all x1, starting transfers between devices, per_device(): lax.all_to_all(buf, ('yh', 'z'), 0, 0, tiled=True)  14.8 us
    dot_general x3, matrix products, dot_hi(): jnp.einsum(form, left, right, precision=lax.Precision.HIGH, preferred_ele...  4.91 us
    all_to_all x1, blocking collectives, per_device(): buf = lax.all_to_all(buf, 'core', 1, 1, tiled=True)  4.79 us
    unnamed x20, local copies, waits for them, and re-layouts  3.38 us
    sin x1, other arithmetic, local_conv(): tab_c, tab_s = lax.optimization_barrier((jnp.cos(angles), jnp.sin(angles)))  2.93 us
    slice x2, local copies, waits for them, and re-layouts, local_conv(): tc, ts = (tab_c[n1_len + n2_len:], tab_s[n1_len + n2_len:])  2.86 us
  transfers between devices with their start and end apart: 1, of which 1 were waited for; matrix products, arithmetic and copies ran while one was open for 9% of the time, Pallas kernels for 0%

profile of v5, /device:TPU:10, one launch (start us, length us, event | category | flops | bytes accessed | tf_op | source)
XLA Modules:
  0.0 111.3 jit_solution(951011060019221424)
XLA Ops:
  0.0 0.0 copy-start
  0.0 1.2 %copy-done = bf16[2,128,2,1024]{3,2,1,0:T(2,128)(2,1)S(1)} copy-done((bf16[2,128,2,1024]{3,2,1,0:T(2,128)(2,1)S(1)}, bf16[2,128,2,1024]{3,2,1,0:T(2,128)(2,1)}, u32[]{:S(2)}) %copy-start) | copy-done | bytes 1048600
  1.2 1.3 %fusion.15 = bf16[2,128,2,1024]{1,3,2,0:T(8,128)(2,1)S(1)} fusion(s32[1024]{0:T(1024)S(1)} %fusion.70, bf16[2,128,2,1024]{3,2,1,0:T(2,128)(2,1)S(1)} %copy-done), kind=kOutput, calls=%fused_computation.20 | convolution fusion | flops 1075314688 | bytes 2101248 | tf_op jit(solution)/shard_map/rcab,bq->rcaq/dot_general | solution.py:78
  2.5 1.0 copy.98
  3.5 0.4 reshape.437
  4.0 0.1 copy.99
  4.1 1.1 %concatenate.30 = bf16[16,2,4,4,256]{4,3,2,1,0:T(4,128)(2,1)S(1)} reshape(bf16[128,1024]{1,0:T(8,128)(2,1)} %param.3) | data formatting | bytes 524288 | tf_op jit(solution)/shard_map/concatenate | solution.py:83
  5.2 0.2 pad_maximum_fusion
  5.4 0.7 copy.100
  6.2 4.8 %all_to_all.15 = bf16[16,2,4,20,256]{4,0,3,2,1:T(8,128)(2,1)S(1)} all-to-all(bf16[16,2,4,20,256]{4,0,3,2,1:T(8,128)(2,1)S(1)} %copy.100), channel_id=1, replica_groups=mesh['yh'=2,'z'=8,'core'=2,'chan'=16] {'core'}, dimensions={1} | all-to-all | bytes 2621440 | tf_op jit(solution)/shard_map/all_to_all | solution.py:86
  11.0 0.0 copy-start.8
  11.0 2.1 %copy.101 = bf16[16,2,4,20,256]{4,2,3,1,0:T(4,128)(2,1)} copy(bf16[16,2,4,20,256]{4,0,3,2,1:T(8,128)(2,1)S(1)} %all_to_all.15) | data formatting | bytes 2621440 | tf_op jit(solution)/shard_map/all_to_all | solution.py:86
  13.1 14.8 %all-to-all-start.1 = ((bf16[16,2,4,20,256]{4,2,3,1,0:T(4,128)(2,1)}), bf16[16,2,4,20,256]{4,2,3,1,0:T(4,128)(2,1)S(1)}, u32[]{:S(2)}, u32[]{:S(2)}) async-start(bf16[16,2,4,20,256]{4,2,3,1,0:T(4,128)(2,1)} %copy.101), calls=%async_computation.1 | async-start | bytes 2621440 | tf_op jit(solution)/shard_map/all_to_all | solution.py:87
  27.9 0.0 copy-done.8
  27.9 0.4 fusion.42
  28.3 2.9 %fusion.36 = (f32[768,256]{1,0:T(8,128)S(1)}, f32[768,256]{1,0:T(8,128)S(1)}) fusion(f32[256,256]{1,0:T(8,128)S(1)} %get-tuple-element.32, f32[256,256]{1,0:T(8,128)S(1)} %get-tuple-element.33, f32[256,256]{1,0:T(8,128)S(1)} %get-tuple-element.31), kind=kLoop, calls=%fused_computation.51 | loop fusion | flops 393216 | bytes 2359296 | tf_op jit(solution)/shard_map/sin | solution.py:35
  31.2 0.0 copy-start.2
  31.3 0.0 copy-start.9
  31.3 0.9 copy-done.2
  32.1 0.8 slice_bitcast_fusion.5
  33.0 1.1 copy.107
  34.0 0.8 slice_bitcast_fusion.4
  34.9 1.8 %copy.108 = f32[256,256]{0,1:T(8,128)} copy(f32[256,256]{1,0:T(8,128)} %get-tuple-element.24) | data formatting | bytes 524288 | tf_op jit(solution)/shard_map/slice | solution.py:38
  36.7 0.0 copy-done.9
  36.7 0.1 dynamic_slice.3
  36.7 0.9 slice_bitcast_fusion.6
  37.7 0.7 fusion.62
  38.3 0.8 reduce-precision_convert_fusion
  39.1 29.3 %all-to-all-done.1 = bf16[16,2,4,20,256]{4,2,3,1,0:T(4,128)(2,1)S(1)} async-done(((bf16[16,2,4,20,256]{4,2,3,1,0:T(4,128)(2,1)}), bf16[16,2,4,20,256]{4,2,3,1,0:T(4,128)(2,1)S(1)}, u32[]{:S(2)}, u32[]{:S(2)}) %all-to-all-start.1) | async-done | bytes 1310752 | tf_op jit(solution)/shard_map/all_to_all | solution.py:87
  68.4 0.1 slice.92
  68.5 0.5 slice.99
  69.1 0.9 convert_bitcast_fusion
  70.0 0.9 copy.103
  70.9 0.6 copy_convert_fusion
  71.5 1.2 %copy.162 = f32[32,4,16,256]{3,2,1,0:T(8,128)S(1)} copy(f32[32,4,16,256]{3,0,2,1:T(8,128)S(1)} %copy_convert_fusion) | data formatting | bytes 4194304 | tf_op jit(solution)/shard_map/transpose | solution.py:91
  72.7 0.3 fusion.81
  73.0 0.2 copy_bitcast_fusion.1
  73.2 1.3 %copy.115 = f32[1,4,256,256]{2,3,1,0:T(8,128)} copy(f32[1,4,256,256]{3,2,1,0:T(8,128)S(1)} %get-tuple-element.35) | data formatting | bytes 2097152 | tf_op jit(solution)/shard_map/squeeze | solution.py:53
  74.6 0.3 copy.117
  74.9 0.0 copy-start.3
  74.9 1.8 %convolution_bitcast_fusion.2 = f32[2,2,4,256,256]{3,4,1,0,2:T(8,128)S(1)} fusion(bf16[1,2,256,128]{3,2,1,0:T(8,128)(2,1)} %get-tuple-element.30, bf16[1,2,256,128]{3,2,1,0:T(8,128)(2,1)} %get-tuple-element.29, bf16[4,128,256,1,1]{2,0,1,4,3:T(4,128)(2,1)} %bitcast.165), kind=kOutput, calls=%fused_computation.5 | convolution fusion | flops 268959744 | bytes 4718592 | tf_op jit(solution)/shard_map/hzkn,cnm->hzckm/dot_general | solution.py:44
  76.7 0.0 copy-done.3
  76.7 0.0 copy-start.4
  76.7 0.0 copy-start.5
  76.8 0.3 multiply_add_fusion.2
  77.1 0.6 copy-done.4
  77.7 0.1 copy-done.5
  77.8 0.0 copy-start.1
  77.8 2.0 %convolution_bitcast_fusion.1 = f32[2,2,4,256,256]{3,4,2,0,1:T(8,128)S(1)} fusion(f32[1,4,256,256]{2,3,1,0:T(8,128)S(1)} %get-tuple-element.14, f32[1,4,256,256]{2,3,1,0:T(8,128)S(1)} %get-tuple-element.13, f32[1,256,256]{2,1,0:T(8,128)S(1)} %copy-done.5, f32[1,256,256]{2,1,0:T(8,128)S(1)} %copy-done.4), kind=kOutput, calls=%fused_computation.4 | convolution fusion | flops 1611268096 | bytes 6815744 | tf_op jit(solution)/shard_map/zckn,wnj->zwckj/dot_general | solution.py:12
  79.8 0.0 copy-done.1
  79.8 0.4 multiply_subtract_fusion.1
  80.2 1.9 %convolution_bitcast_fusion = f32[2,2,4,256,256]{3,4,2,1,0:T(8,128)S(1)} fusion(f32[1,4,256,256]{2,3,1,0:T(8,128)S(1)} %get-tuple-element.10, f32[1,4,256,256]{2,3,1,0:T(8,128)S(1)} %get-tuple-element.9, f32[1,256,256]{2,1,0:T(8,128)S(1)} %copy-done.5, f32[1,256,256]{2,1,0:T(8,128)S(1)} %copy-done.4), kind=kOutput, calls=%fused_computation.3 | convolution fusion | flops 1611268096 | bytes 6815744 | tf_op jit(solution)/shard_map/zckj,wjn->zwckn/dot_general | solution.py:12
  82.1 0.0 copy-start.7
  82.1 0.3 multiply_subtract_fusion
  82.5 0.6 copy-done.7
  83.0 0.0 copy-start.6
  83.0 1.0 fusion.24
  84.0 0.2 copy.123
  84.2 0.1 mul.286
  84.4 0.0 copy-done.6
  84.5 0.1 fusion.50
  84.6 0.2 copy.125
  84.8 25.7 %all_to_all.16 = bf16[32,4,1024]{2,1,0:T(4,128)(2,1)S(1)} all-to-all(bf16[32,4,1024]{2,1,0:T(4,128)(2,1)S(1)} %copy.125), channel_id=1, replica_groups=mesh['yh'=2,'z'=8,'core'=2,'chan'=16] {'yh','z','core'}, dimensions={0} | all-to-all | bytes 524288 | tf_op jit(solution)/shard_map/all_to_all | solution.py:95
  110.5 0.8 reshape.439
  (3 shorter events, 0.1 us)
Async XLA Ops:
  0.0 1.2 %copy-start = (bf16[2,128,2,1024]{3,2,1,0:T(2,128)(2,1)S(1)}, bf16[2,128,2,1024]{3,2,1,0:T(2,128)(2,1)}, u32[]{:S(2)}) copy-start(bf16[2,128,2,1024]{3,2,1,0:T(2,128)(2,1)} %param.4) | copy-start | bytes 3145732
  11.0 16.9 %copy-start.8 = (s32[256]{0:T(256)S(1)}, s32[256]{0:T(256)}, u32[]{:S(2)}) copy-start(s32[256]{0:T(256)} %constant.100.clone.1) | copy-start | bytes 3076
  13.1 55.4 %all-to-all-start.1 = ((bf16[16,2,4,20,256]{4,2,3,1,0:T(4,128)(2,1)}), bf16[16,2,4,20,256]{4,2,3,1,0:T(4,128)(2,1)S(1)}, u32[]{:S(2)}, u32[]{:S(2)}) async-start(bf16[16,2,4,20,256]{4,2,3,1,0:T(4,128)(2,1)} %copy.101), calls=%async_computation.1 | async-start | bytes 2621440 | tf_op jit(solution)/shard_map/all_to_all | solution.py:87
  31.2 0.9 copy-start.2
  31.3 5.4 %copy-start.9 = (f32[128]{0:T(128)S(1)}, f32[128]{0:T(128)}, u32[]{:S(2)}) copy-start(f32[128]{0:T(128)} %param.5) | copy-start | bytes 1540
  74.9 1.8 %copy-start.3 = (f32[256,256]{0,1:T(8,128)S(1)}, f32[256,256]{0,1:T(8,128)}, u32[]{:S(2)}) copy-start(f32[256,256]{0,1:T(8,128)} %copy.108) | copy-start | bytes 786436
  76.7 1.0 copy-start.4
  76.7 1.0 copy-start.5
  77.8 2.0 %copy-start.1 = (f32[1,4,256,256]{2,3,1,0:T(8,128)S(1)}, f32[1,4,256,256]{2,3,1,0:T(8,128)}, u32[]{:S(2)}) copy-start(f32[1,4,256,256]{2,3,1,0:T(8,128)} %copy.115) | copy-start | bytes 3145732
  82.1 0.9 copy-start.7
  83.0 1.4 %copy-start.6 = (f32[4,4,4,8,256]{4,3,2,1,0:T(8,128)S(1)}, f32[4,4,4,8,256]{4,3,2,1,0:T(8,128)}, u32[]{:S(2)}) copy-start(f32[4,4,4,8,256]{4,3,2,1,0:T(8,128)} %get-tuple-element.27) | copy-start | bytes 1572868

commit v6 on v3

--- a/solution.py
+++ b/solution.py
@@ -82,8 +82,9 @@
     got = lax.all_to_all(buf, "seq", 0, 0, tiled=True)
     spec_rows = 2 * a_loc * rep
     x = got[:, :, spec_rows:].transpose(1, 0, 2, 3).reshape(cpd, parts * slab)
-    s = got[:, :, :spec_rows].reshape(parts, cpd, 2, a_loc * rep, n2_len).astype(jnp.float32)
-    s = s.transpose(2, 1, 0, 3, 4).reshape(2, cpd, n1_len, n2_len)
+    half_rows = spec_rows // 2
+    s = [got[:, :, h * half_rows:(h + 1) * half_rows].astype(jnp.float32)
+         .transpose(1, 0, 2, 3).reshape(cpd, n1_len, n2_len) for h in range(2)]
     gain = lax.dynamic_slice_in_dim(skip_gain, seq_rank * cpd, cpd)
     out = local_conv(x, s, gain, n1_len, km)
     back = out.reshape(cpd, parts, slab).transpose(1, 0, 2)

time: 96.9 us -> 96.3 us (level)
  waiting for transfers between devices: 28.4 us -> 27.3 us
    squeeze x3 -> x0, local copies, waits for them, and re-layouts: 1.86 us -> none  [local_conv(): pr = xfr * s[0] - xfi * s[1]]
    reshape x0 -> x2, local copies, waits for them, and re-layouts: none -> 1.66 us  [per_device(): s = [got[:, :, h * half_rows:(h + 1) * half_rows].astype(jnp.float32).tra...]
    all_to_all x1, waiting for transfers between devices: 28.4 us -> 27.3 us  [per_device(): got = lax.all_to_all(buf, 'seq', 0, 0, tiled=True)]
    another operation x2, local copies, waits for them, and re-layouts: 1.66 us -> 2.69 us  [local_conv(): w = jnp.stack([wc, ws])]
    sin x1, other arithmetic: 2.75 us -> 3.78 us  [local_conv(): tab_c, tab_s = lax.optimization_barrier((jnp.cos(angles), jnp.sin(angles)))]
    unnamed x22 -> x20, local copies, waits for them, and re-layouts: 3.79 us -> 2.93 us
  transfers between devices with their start and end apart: 1 -> 1, of which waited for: 1 -> 1; matrix products, arithmetic and copies ran while one was open for 11% -> 13% of each run, Pallas kernels for 0% -> 0%
where the time goes in v6:
time: 96.3 us; the launch traced here: 95.9 us
  waiting for transfers between devices  27.3 us (28%)
  blocking collectives  19.6 us (20%)
  local copies, waits for them, and re-layouts  17.4 us (18%)
  starting transfers between devices  15.2 us (16%)
  other arithmetic  8.12 us (8%)
  matrix products  8.02 us (8%)
    all_to_all x1, waiting for transfers between devices, per_device(): got = lax.all_to_all(buf, 'seq', 0, 0, tiled=True)  27.3 us
    all_to_all x1, blocking collectives, per_device(): back = lax.all_to_all(back, 'seq', 0, 0, tiled=True)  19.6 us
    all_to_all x1, starting transfers between devices, per_device(): got = lax.all_to_all(buf, 'seq', 0, 0, tiled=True)  15.2 us
    dot_general x3, matrix products, dot_hi(): jnp.einsum(form, left, right, precision=lax.Precision.HIGH, preferred_ele...  4.91 us
    sin x1, other arithmetic, local_conv(): tab_c, tab_s = lax.optimization_barrier((jnp.cos(angles), jnp.sin(angles)))  3.78 us
    unnamed x20, local copies, waits for them, and re-layouts  2.93 us
    slice x2, local copies, waits for them, and re-layouts, local_conv(): tc, ts = (tab_c[n1_len + n2_len:], tab_s[n1_len + n2_len:])  2.86 us
    another operation x2, local copies, waits for them, and re-layouts, local_conv(): w = jnp.stack([wc, ws])  2.69 us
  transfers between devices with their start and end apart: 1, of which 1 were waited for; matrix products, arithmetic and copies ran while one was open for 13% of the time, Pallas kernels for 0%

profile of v6, /device:TPU:14, one launch (start us, length us, event | category | flops | bytes accessed | tf_op | source)
XLA Modules:
  0.0 95.9 jit_solution(4245182778002074047)
XLA Ops:
  0.0 0.0 copy-start
  0.0 1.2 %copy-done = bf16[2,128,2,1024]{3,2,1,0:T(2,128)(2,1)S(1)} copy-done((bf16[2,128,2,1024]{3,2,1,0:T(2,128)(2,1)S(1)}, bf16[2,128,2,1024]{3,2,1,0:T(2,128)(2,1)}, u32[]{:S(2)}) %copy-start) | copy-done | bytes 1048600
  1.2 1.3 %fusion.15 = bf16[2,128,2,1024]{1,3,2,0:T(8,128)(2,1)S(1)} fusion(s32[1024]{0:T(1024)S(1)} %fusion.70, bf16[2,128,2,1024]{3,2,1,0:T(2,128)(2,1)S(1)} %copy-done), kind=kOutput, calls=%fused_computation.19 | convolution fusion | flops 1075314688 | bytes 2101248 | tf_op jit(solution)/shard_map/rcab,bq->rcaq/dot_general | solution.py:76
  2.5 1.0 %copy.91 = bf16[2,128,2,1024]{3,2,1,0:T(2,128)(2,1)S(1)} copy(bf16[2,128,2,1024]{1,3,2,0:T(8,128)(2,1)S(1)} %fusion.15) | data formatting | bytes 2097152 | tf_op jit(solution)/shard_map/convert_element_type | solution.py:77
  3.5 0.0 copy-start.7
  3.5 0.4 reshape.437
  4.0 0.1 copy_bitcast_fusion
  4.1 0.4 copy-done.7
  4.5 0.2 reshape.439
  4.7 0.2 pad_maximum_fusion
  4.9 0.0 copy-start.8
  4.9 1.6 %copy.93 = bf16[32,4,20,256]{3,1,2,0:T(4,128)(2,1)} copy(bf16[32,4,20,256]{3,2,1,0:T(8,128)(2,1)S(1)} %pad_maximum_fusion) | data formatting | bytes 2621440 | tf_op jit(solution)/shard_map/concatenate | solution.py:81
  6.5 15.2 %all-to-all-start = ((bf16[32,4,20,256]{3,1,2,0:T(4,128)(2,1)}), bf16[32,4,20,256]{3,1,2,0:T(4,128)(2,1)S(1)}, u32[]{:S(2)}, u32[]{:S(2)}) async-start(bf16[32,4,20,256]{3,1,2,0:T(4,128)(2,1)} %copy.93), calls=%async_computation | async-start | bytes 2621440 | tf_op jit(solution)/shard_map/all_to_all | solution.py:82
  21.8 0.0 copy-done.8
  21.8 0.4 fusion.42
  22.2 3.8 %fusion.36 = (f32[768,256]{1,0:T(8,128)S(1)}, f32[768,256]{1,0:T(8,128)}) fusion(f32[256,256]{1,0:T(8,128)S(1)} %get-tuple-element.32, f32[256,256]{1,0:T(8,128)S(1)} %get-tuple-element.33, f32[256,256]{1,0:T(8,128)S(1)} %get-tuple-element.31), kind=kLoop, calls=%fused_computation.50 | loop fusion | flops 393216 | bytes 2359296 | tf_op jit(solution)/shard_map/sin | solution.py:33
  26.0 0.0 copy-start.9
  26.0 0.8 slice_bitcast_fusion.4
  26.8 1.1 %copy.100 = f32[256,256]{0,1:T(8,128)S(1)} copy(f32[256,256]{1,0:T(8,128)} %get-tuple-element.24) | data formatting | bytes 524288 | tf_op jit(solution)/shard_map/slice | solution.py:36
  27.9 1.9 %slice_bitcast_fusion.5 = (f32[1,256,256]{2,1,0:T(8,128)}, f32[256,256]{1,0:T(8,128)}) fusion(f32[768,256]{1,0:T(8,128)} %get-tuple-element.7), kind=kLoop, calls=%fused_computation.91 | loop fusion | bytes 1048576 | tf_op jit(solution)/shard_map/stack | solution.py:47
  29.8 1.8 %copy.99 = f32[256,256]{0,1:T(8,128)} copy(f32[256,256]{1,0:T(8,128)} %get-tuple-element.22) | data formatting | bytes 524288 | tf_op jit(solution)/shard_map/slice | solution.py:36
  31.5 0.0 copy-done.9
  31.5 0.1 dynamic_slice.3
  31.6 0.9 slice_bitcast_fusion.6
  32.5 0.7 fusion.62
  33.2 0.8 reduce-precision_convert_fusion
  34.0 27.3 %all-to-all-done = bf16[32,4,20,256]{3,1,2,0:T(4,128)(2,1)S(1)} async-done(((bf16[32,4,20,256]{3,1,2,0:T(4,128)(2,1)}), bf16[32,4,20,256]{3,1,2,0:T(4,128)(2,1)S(1)}, u32[]{:S(2)}, u32[]{:S(2)}) %all-to-all-start) | async-done | bytes 1310752 | tf_op jit(solution)/shard_map/all_to_all | solution.py:82
  61.2 0.1 slice.84
  61.3 0.9 convert_bitcast_fusion.2
  62.2 0.9 copy.95
  63.1 0.6 fusion.81
  63.7 0.2 convert_bitcast_fusion
  63.9 1.3 %copy.106 = f32[1,4,256,256]{2,3,1,0:T(8,128)} copy(f32[1,4,256,256]{3,2,1,0:T(8,128)S(1)} %get-tuple-element.35) | data formatting | bytes 2097152 | tf_op jit(solution)/shard_map/reshape | solution.py:87
  65.3 0.3 copy.108
  65.6 0.0 copy-start.2
  65.6 1.8 %convolution_bitcast_fusion.2 = f32[2,2,4,256,256]{3,4,1,0,2:T(8,128)S(1)} fusion(bf16[1,2,256,128]{3,2,1,0:T(8,128)(2,1)} %get-tuple-element.30, bf16[1,2,256,128]{3,2,1,0:T(8,128)(2,1)} %get-tuple-element.29, bf16[4,128,256,1,1]{2,0,1,4,3:T(4,128)(2,1)} %bitcast.161), kind=kOutput, calls=%fused_computation.5 | convolution fusion | flops 268959744 | bytes 4718592 | tf_op jit(solution)/shard_map/hzkn,cnm->hzckm/dot_general | solution.py:42
  67.4 0.0 copy-done.2
  67.4 0.0 copy-start.3
  67.5 0.0 copy-start.4
  67.5 0.3 multiply_add_fusion.2
  67.8 0.6 copy-done.3
  68.4 0.1 copy-done.4
  68.5 0.0 copy-start.1
  68.5 2.0 %convolution_bitcast_fusion.1 = f32[2,2,4,256,256]{3,4,2,0,1:T(8,128)S(1)} fusion(f32[1,4,256,256]{2,3,1,0:T(8,128)S(1)} %get-tuple-element.14, f32[1,4,256,256]{2,3,1,0:T(8,128)S(1)} %get-tuple-element.13, f32[1,256,256]{2,1,0:T(8,128)S(1)} %copy-done.3, f32[1,256,256]{2,1,0:T(8,128)S(1)} %copy-done.4), kind=kOutput, calls=%fused_computation.4 | convolution fusion | flops 1611268096 | bytes 6815744 | tf_op jit(solution)/shard_map/zckn,wnj->zwckj/dot_general | solution.py:10
  70.5 0.0 copy-done.1
  70.5 0.4 multiply_subtract_fusion.1
  70.9 1.9 %convolution_bitcast_fusion = f32[2,2,4,256,256]{3,4,2,1,0:T(8,128)S(1)} fusion(f32[1,4,256,256]{2,3,1,0:T(8,128)S(1)} %get-tuple-element.10, f32[1,4,256,256]{2,3,1,0:T(8,128)S(1)} %get-tuple-element.9, f32[1,256,256]{2,1,0:T(8,128)S(1)} %copy-done.3, f32[1,256,256]{2,1,0:T(8,128)S(1)} %copy-done.4), kind=kOutput, calls=%fused_computation.3 | convolution fusion | flops 1611268096 | bytes 6815744 | tf_op jit(solution)/shard_map/zckj,wjn->zwckn/dot_general | solution.py:10
  72.8 0.0 copy-start.6
  72.9 0.3 multiply_subtract_fusion
  73.2 0.6 copy-done.6
  73.7 0.0 copy-start.5
  73.7 1.0 %fusion.24 = f32[4,128,256]{1,2,0:T(8,128)S(1)} fusion(f32[1,4,256,256]{2,3,1,0:T(8,128)S(1)} %get-tuple-element.12, f32[1,4,256,256]{2,3,1,0:T(8,128)S(1)} %get-tuple-element.11, f32[1,256,128]{2,1,0:T(8,128)S(1)} %copy-done.6, f32[1,256,128]{2,1,0:T(8,128)S(1)} %get-tuple-element.17), kind=kOutput, calls=%fused_computation.22 | convolution fusion | flops 403374080 | bytes 2883584 | tf_op jit(solution)/shard_map/zkn,zckm->cnm/dot_general | solution.py:10
  74.7 0.2 copy.114
  75.0 0.1 mul.280
  75.1 0.0 copy-done.5
  75.2 0.1 fusion.50
  75.3 0.2 copy.116
  75.5 19.6 %all_to_all.10 = bf16[32,4,1024]{2,1,0:T(4,128)(2,1)S(1)} all-to-all(bf16[32,4,1024]{2,1,0:T(4,128)(2,1)S(1)} %copy.116), channel_id=1, replica_groups=mesh['seq'=32,'chan'=16] {'seq'}, dimensions={0} | all-to-all | bytes 524288 | tf_op jit(solution)/shard_map/all_to_all | solution.py:91
  95.1 0.8 reshape.444
  (3 shorter events, 0.1 us)
Async XLA Ops:
  0.0 1.2 %copy-start = (bf16[2,128,2,1024]{3,2,1,0:T(2,128)(2,1)S(1)}, bf16[2,128,2,1024]{3,2,1,0:T(2,128)(2,1)}, u32[]{:S(2)}) copy-start(bf16[2,128,2,1024]{3,2,1,0:T(2,128)(2,1)} %param.4) | copy-start | bytes 3145732
  3.5 1.0 copy-start.7
  4.9 16.9 %copy-start.8 = (s32[256]{0:T(256)S(1)}, s32[256]{0:T(256)}, u32[]{:S(2)}) copy-start(s32[256]{0:T(256)} %constant.91.clone.1) | copy-start | bytes 3076
  6.5 54.8 %all-to-all-start = ((bf16[32,4,20,256]{3,1,2,0:T(4,128)(2,1)}), bf16[32,4,20,256]{3,1,2,0:T(4,128)(2,1)S(1)}, u32[]{:S(2)}, u32[]{:S(2)}) async-start(bf16[32,4,20,256]{3,1,2,0:T(4,128)(2,1)} %copy.93), calls=%async_computation | async-start | bytes 2621440 | tf_op jit(solution)/shard_map/all_to_all | solution.py:82
  26.0 5.6 %copy-start.9 = (f32[128]{0:T(128)S(1)}, f32[128]{0:T(128)}, u32[]{:S(2)}) copy-start(f32[128]{0:T(128)} %param.5) | copy-start | bytes 1540
  65.6 1.8 %copy-start.2 = (f32[256,256]{0,1:T(8,128)S(1)}, f32[256,256]{0,1:T(8,128)}, u32[]{:S(2)}) copy-start(f32[256,256]{0,1:T(8,128)} %copy.99) | copy-start | bytes 786436
  67.4 1.0 copy-start.3
  67.5 1.0 %copy-start.4 = (f32[1,256,256]{2,1,0:T(8,128)S(1)}, f32[1,256,256]{2,1,0:T(8,128)}, u32[]{:S(2)}) copy-start(f32[1,256,256]{2,1,0:T(8,128)} %get-tuple-element.21) | copy-start | bytes 786436
  68.5 2.0 %copy-start.1 = (f32[1,4,256,256]{2,3,1,0:T(8,128)S(1)}, f32[1,4,256,256]{2,3,1,0:T(8,128)}, u32[]{:S(2)}) copy-start(f32[1,4,256,256]{2,3,1,0:T(8,128)} %copy.106) | copy-start | bytes 3145732
  72.8 0.9 copy-start.6
  73.7 1.4 %copy-start.5 = (f32[4,4,4,8,256]{4,3,2,1,0:T(8,128)S(1)}, f32[4,4,4,8,256]{4,3,2,1,0:T(8,128)}, u32[]{:S(2)}) copy-start(f32[4,4,4,8,256]{4,3,2,1,0:T(8,128)} %get-tuple-element.27) | copy-start | bytes 1572868

commit v7 on v4

--- a/solution.py
+++ b/solution.py
@@ -16,7 +16,7 @@
 
 
 def local_conv(x, s, gain, n1_len, km):
-    n2_len = s.shape[3]
+    n2_len = s[0].shape[2]
     parts, count = x.shape[0], x.shape[1]
     length = parts * x.shape[2] * x.shape[3]
     full_len = 2 * length
@@ -84,8 +84,9 @@
     got = lax.all_to_all(buf, "seq", 0, 0, tiled=True)
     spec_rows = 2 * a_loc * rep
     x = got[:, :, spec_rows:]
-    s = got[:, :, :spec_rows].reshape(parts, cpd, 2, a_loc * rep, n2_len).astype(jnp.float32)
-    s = s.transpose(2, 1, 0, 3, 4).reshape(2, cpd, n1_len, n2_len)
+    half_rows = spec_rows // 2
+    s = [got[:, :, h * half_rows:(h + 1) * half_rows].astype(jnp.float32)
+         .transpose(1, 0, 2, 3).reshape(cpd, n1_len, n2_len) for h in range(2)]
     gain = lax.dynamic_slice_in_dim(skip_gain, seq_rank * cpd, cpd)
     out = local_conv(x, s, gain, n1_len, km)
     back = out.reshape(cpd, parts, slab).transpose(1, 0, 2)

time: 98.2 us -> 97.6 us (level)
  local copies, waits for them, and re-layouts: 18.9 us -> 17.5 us
    squeeze x3 -> x0, local copies, waits for them, and re-layouts: 5.03 us -> none  [local_conv(): pr = xfr * s[0] - xfi * s[1]]
    reshape x0 -> x2, local copies, waits for them, and re-layouts: none -> 3.87 us  [per_device(): s = [got[:, :, h * half_rows:(h + 1) * half_rows].astype(jnp.float32).tra...]
    reshape x0 -> x1, other arithmetic: none -> 1.16 us  [per_device(): s = [got[:, :, h * half_rows:(h + 1) * half_rows].astype(jnp.float32).tra...]
where the time goes in v7:
time: 97.6 us; the launch traced here: 97.2 us
  waiting for transfers between devices  29.4 us (30%)
  blocking collectives  19.6 us (20%)
  local copies, waits for them, and re-layouts  17.5 us (18%)
  starting transfers between devices  15.2 us (16%)
  matrix products  7.85 us (8%)
  other arithmetic  7.3 us (7%)
    all_to_all x1, waiting for transfers between devices, per_device(): got = lax.all_to_all(buf, 'seq', 0, 0, tiled=True)  29.4 us
    all_to_all x1, blocking collectives, per_device(): back = lax.all_to_all(back, 'seq', 0, 0, tiled=True)  19.6 us
    all_to_all x1, starting transfers between devices, per_device(): got = lax.all_to_all(buf, 'seq', 0, 0, tiled=True)  15.2 us
    dot_general x3, matrix products, dot_hi(): jnp.einsum(form, left, right, precision=lax.Precision.HIGH, preferred_ele...  4.8 us
    reshape x2, local copies, waits for them, and re-layouts, per_device(): s = [got[:, :, h * half_rows:(h + 1) * half_rows].astype(jnp.float32).tra...  3.87 us
    unnamed x25, local copies, waits for them, and re-layouts  3.83 us
    sin x1, other arithmetic, local_conv(): tab_c, tab_s = lax.optimization_barrier((jnp.cos(angles), jnp.sin(angles)))  2.8 us
    another operation x2, local copies, waits for them, and re-layouts, local_conv(): w = jnp.stack([wc, ws])  2.7 us
  transfers between devices with their start and end apart: 1, of which 1 were waited for; matrix products, arithmetic and copies ran while one was open for 9% of the time, Pallas kernels for 0%

profile of v7, /device:TPU:14, one launch (start us, length us, event | category | flops | bytes accessed | tf_op | source)
XLA Modules:
  0.0 97.2 jit_solution(242368273493975537)
XLA Ops:
  0.0 0.0 copy-start
  0.0 1.2 %copy-done = bf16[2,128,2,1024]{3,2,1,0:T(2,128)(2,1)S(1)} copy-done((bf16[2,128,2,1024]{3,2,1,0:T(2,128)(2,1)S(1)}, bf16[2,128,2,1024]{3,2,1,0:T(2,128)(2,1)}, u32[]{:S(2)}) %copy-start) | copy-done | bytes 1048600
  1.2 1.3 %fusion.15 = bf16[2,128,2,1024]{1,3,2,0:T(8,128)(2,1)S(1)} fusion(s32[1024]{0:T(1024)S(1)} %fusion.69, bf16[2,128,2,1024]{3,2,1,0:T(2,128)(2,1)S(1)} %copy-done), kind=kOutput, calls=%fused_computation.19 | convolution fusion | flops 1075314688 | bytes 2101248 | tf_op jit(solution)/shard_map/rcab,bq->rcaq/dot_general | solution.py:78
  2.5 1.0 %copy.107 = bf16[2,128,2,1024]{3,2,1,0:T(2,128)(2,1)S(1)} copy(bf16[2,128,2,1024]{1,3,2,0:T(8,128)(2,1)S(1)} %fusion.15) | data formatting | bytes 2097152 | tf_op jit(solution)/shard_map/convert_element_type | solution.py:79
  3.5 0.0 copy-start.9
  3.5 0.4 reshape.448
  4.0 0.1 copy_bitcast_fusion
  4.1 0.4 copy-done.9
  4.5 0.2 reshape.450
  4.7 0.2 pad_maximum_fusion
  4.9 0.0 copy-start.10
  4.9 1.6 %copy.109 = bf16[32,4,20,256]{3,1,2,0:T(4,128)(2,1)} copy(bf16[32,4,20,256]{3,2,1,0:T(8,128)(2,1)S(1)} %pad_maximum_fusion) | data formatting | bytes 2621440 | tf_op jit(solution)/shard_map/concatenate | solution.py:83
  6.5 15.2 %all-to-all-start = ((bf16[32,4,20,256]{3,1,2,0:T(4,128)(2,1)}), bf16[32,4,20,256]{3,1,2,0:T(4,128)(2,1)S(1)}, u32[]{:S(2)}, u32[]{:S(2)}) async-start(bf16[32,4,20,256]{3,1,2,0:T(4,128)(2,1)} %copy.109), calls=%async_computation | async-start | bytes 2621440 | tf_op jit(solution)/shard_map/all_to_all | solution.py:84
  21.8 0.0 copy-done.10
  21.8 0.0 copy-start.11
  21.8 0.4 fusion.42
  22.2 2.8 %fusion.36 = (f32[768,256]{0,1:T(8,128)S(1)}, f32[768,256]{0,1:T(8,128)S(1)}) fusion(f32[256,256]{0,1:T(8,128)S(1)} %get-tuple-element.30, f32[256,256]{0,1:T(8,128)S(1)} %get-tuple-element.31, f32[256,256]{0,1:T(8,128)S(1)} %get-tuple-element.29), kind=kLoop, calls=%fused_computation.50 | loop fusion | flops 393216 | bytes 2359296 | tf_op jit(solution)/shard_map/sin | solution.py:34
  25.0 0.0 copy-start.3
  25.0 0.9 copy-done.3
  26.0 0.7 fusion.80
  26.6 0.7 stack.51
  27.3 0.0 copy-done.11
  27.3 0.1 dynamic_slice.3
  27.4 0.9 copy_dynamic-update-slice_fusion
  28.4 1.9 %slice_bitcast_fusion.5 = (f32[1,256,256]{1,2,0:T(8,128)}, f32[256,256]{0,1:T(8,128)}) fusion(f32[768,256]{0,1:T(8,128)} %copy-done.3), kind=kLoop, calls=%fused_computation.89 | loop fusion | bytes 1048576 | tf_op jit(solution)/shard_map/stack | solution.py:48
  30.2 0.8 slice_bitcast_fusion.4
  31.1 0.7 reduce-precision_convert_fusion
  31.8 29.4 %all-to-all-done = bf16[32,4,20,256]{3,1,2,0:T(4,128)(2,1)S(1)} async-done(((bf16[32,4,20,256]{3,1,2,0:T(4,128)(2,1)}), bf16[32,4,20,256]{3,1,2,0:T(4,128)(2,1)S(1)}, u32[]{:S(2)}, u32[]{:S(2)}) %all-to-all-start) | async-done | bytes 1310752 | tf_op jit(solution)/shard_map/all_to_all | solution.py:84
  61.2 0.6 fusion.81
  61.8 1.2 %convert_bitcast_fusion = (f32[1,4,256,256]{3,2,1,0:T(8,128)S(1)}, f32[1,4,256,256]{3,2,1,0:T(8,128)}) fusion(bf16[32,4,8,256]{3,1,2,0:T(4,128)(2,1)S(1)} %get-tuple-element.15, bf16[32,4,8,256]{3,1,2,0:T(4,128)(2,1)S(1)} %get-tuple-element.16), kind=kLoop, calls=%fused_computation.41 | loop fusion | flops 524288 | bytes 3145728 | tf_op jit(solution)/shard_map/reshape | solution.py:89
  63.0 2.6 %copy.119 = f32[1,4,256,256]{2,3,1,0:T(8,128)} copy(f32[1,4,256,256]{3,2,1,0:T(8,128)} %get-tuple-element.33) | data formatting | bytes 2097152 | tf_op jit(solution)/shard_map/reshape | solution.py:89
  65.6 1.3 %copy.121 = f32[1,4,256,256]{2,3,1,0:T(8,128)} copy(f32[1,4,256,256]{3,2,1,0:T(8,128)S(1)} %get-tuple-element.32) | data formatting | bytes 2097152 | tf_op jit(solution)/shard_map/reshape | solution.py:89
  66.9 0.1 slice.84
  67.0 0.1 convert_bitcast_fusion.2
  67.1 0.0 copy-start.4
  67.1 0.0 copy-start.5
  67.1 1.8 %convolution_bitcast_fusion.2 = f32[2,2,4,256,256]{3,4,1,0,2:T(8,128)S(1)} fusion(bf16[1,2,256,32,4]{2,3,4,1,0:T(8,128)(2,1)} %get-tuple-element.28, bf16[1,2,256,32,4]{2,3,4,1,0:T(8,128)(2,1)} %get-tuple-element.27, bf16[32,4,4,256]{3,1,2,0:T(4,128)(2,1)S(1)} %slice.84), kind=kOutput, calls=%fused_computation.5 | convolution fusion | flops 268959744 | bytes 4718592 | tf_op jit(solution)/shard_map/hzkpi,pcim->hzckm/dot_general | solution.py:44
  68.8 0.0 copy-done.4
  68.9 0.0 copy-done.5
  68.9 0.0 copy-start.6
  68.9 0.0 copy-start.7
  68.9 0.3 multiply_add_fusion.2
  69.2 0.6 copy-done.6
  69.8 0.1 copy-done.7
  69.9 0.0 copy-start.1
  69.9 0.0 copy-start.2
  69.9 1.9 %convolution_bitcast_fusion.1 = f32[2,2,4,256,256]{3,4,2,0,1:T(8,128)S(1)} fusion(f32[1,4,256,256]{2,3,1,0:T(8,128)S(1)} %get-tuple-element.14, f32[1,4,256,256]{2,3,1,0:T(8,128)S(1)} %get-tuple-element.13, f32[1,256,256]{1,2,0:T(8,128)S(1)} %copy-done.7, f32[1,256,256]{1,2,0:T(8,128)S(1)} %copy-done.6), kind=kOutput, calls=%fused_computation.4 | convolution fusion | flops 1611268096 | bytes 6815744 | tf_op jit(solution)/shard_map/zckn,wnj->zwckj/dot_general | solution.py:10
  71.8 0.0 copy-done.1
  71.9 0.0 copy-done.2
  71.9 0.4 multiply_subtract_fusion.1
  72.3 1.9 %convolution_bitcast_fusion = f32[2,2,4,256,256]{3,4,2,1,0:T(8,128)S(1)} fusion(f32[1,4,256,256]{2,3,1,0:T(8,128)S(1)} %get-tuple-element.10, f32[1,4,256,256]{2,3,1,0:T(8,128)S(1)} %get-tuple-element.9, f32[1,256,256]{1,2,0:T(8,128)S(1)} %copy-done.7, f32[1,256,256]{1,2,0:T(8,128)S(1)} %copy-done.6), kind=kOutput, calls=%fused_computation.3 | convolution fusion | flops 1611268096 | bytes 6815744 | tf_op jit(solution)/shard_map/zckj,wjn->zwckn/dot_general | solution.py:10
  74.2 0.0 copy-start.8
  74.2 0.3 multiply_subtract_fusion
  74.5 0.6 copy-done.8
  75.1 1.0 %fusion.24 = f32[4,128,256]{1,2,0:T(8,128)S(1)} fusion(f32[1,4,256,256]{2,3,1,0:T(8,128)S(1)} %get-tuple-element.12, f32[1,4,256,256]{2,3,1,0:T(8,128)S(1)} %get-tuple-element.11, f32[1,256,128]{1,2,0:T(8,128)S(1)} %copy-done.8, f32[1,256,128]{1,2,0:T(8,128)S(1)} %get-tuple-element.17), kind=kOutput, calls=%fused_computation.22 | convolution fusion | flops 403374080 | bytes 2883584 | tf_op jit(solution)/shard_map/zkn,zckm->cnm/dot_general | solution.py:10
  76.1 0.2 copy.127
  76.3 0.1 mul.280
  76.5 0.1 fusion.50
  76.6 0.2 copy.129
  76.8 19.6 %all_to_all.10 = bf16[32,4,1024]{2,1,0:T(4,128)(2,1)S(1)} all-to-all(bf16[32,4,1024]{2,1,0:T(4,128)(2,1)S(1)} %copy.129), channel_id=1, replica_groups=mesh['seq'=32,'chan'=16] {'seq'}, dimensions={0} | all-to-all | bytes 524288 | tf_op jit(solution)/shard_map/all_to_all | solution.py:93
  96.4 0.8 reshape.455
  (6 shorter events, 0.1 us)
Async XLA Ops:
  0.0 1.2 %copy-start = (bf16[2,128,2,1024]{3,2,1,0:T(2,128)(2,1)S(1)}, bf16[2,128,2,1024]{3,2,1,0:T(2,128)(2,1)}, u32[]{:S(2)}) copy-start(bf16[2,128,2,1024]{3,2,1,0:T(2,128)(2,1)} %param.4) | copy-start | bytes 3145732
  3.5 1.0 copy-start.9
  4.9 16.9 %copy-start.10 = (s32[256]{0:T(256)S(1)}, s32[256]{0:T(256)}, u32[]{:S(2)}) copy-start(s32[256]{0:T(256)} %constant.91.clone.1) | copy-start | bytes 3076
  6.5 54.8 %all-to-all-start = ((bf16[32,4,20,256]{3,1,2,0:T(4,128)(2,1)}), bf16[32,4,20,256]{3,1,2,0:T(4,128)(2,1)S(1)}, u32[]{:S(2)}, u32[]{:S(2)}) async-start(bf16[32,4,20,256]{3,1,2,0:T(4,128)(2,1)} %copy.109), calls=%async_computation | async-start | bytes 2621440 | tf_op jit(solution)/shard_map/all_to_all | solution.py:84
  21.8 5.6 %copy-start.11 = (f32[128]{0:T(128)S(1)}, f32[128]{0:T(128)}, u32[]{:S(2)}) copy-start(f32[128]{0:T(128)} %param.5) | copy-start | bytes 1540
  25.0 0.9 copy-start.3
  67.1 1.8 %copy-start.4 = (f32[256,256]{0,1:T(8,128)S(1)}, f32[256,256]{0,1:T(8,128)}, u32[]{:S(2)}) copy-start(f32[256,256]{0,1:T(8,128)} %get-tuple-element.22) | copy-start | bytes 786436
  67.1 1.8 %copy-start.5 = (f32[256,256]{0,1:T(8,128)S(1)}, f32[256,256]{0,1:T(8,128)}, u32[]{:S(2)}) copy-start(f32[256,256]{0,1:T(8,128)} %get-tuple-element.24) | copy-start | bytes 786436
  68.9 1.0 copy-start.6
  68.9 1.0 %copy-start.7 = (f32[1,256,256]{1,2,0:T(8,128)S(1)}, f32[1,256,256]{1,2,0:T(8,128)}, u32[]{:S(2)}) copy-start(f32[1,256,256]{1,2,0:T(8,128)} %get-tuple-element.23) | copy-start | bytes 786436
  69.9 2.0 %copy-start.1 = (f32[1,4,256,256]{2,3,1,0:T(8,128)S(1)}, f32[1,4,256,256]{2,3,1,0:T(8,128)}, u32[]{:S(2)}) copy-start(f32[1,4,256,256]{2,3,1,0:T(8,128)} %copy.119) | copy-start | bytes 3145732
  69.9 2.0 %copy-start.2 = (f32[1,4,256,256]{2,3,1,0:T(8,128)S(1)}, f32[1,4,256,256]{2,3,1,0:T(8,128)}, u32[]{:S(2)}) copy-start(f32[1,4,256,256]{2,3,1,0:T(8,128)} %copy.121) | copy-start | bytes 3145732
  74.2 0.9 copy-start.8

commit v8 on v6

--- a/solution.py
+++ b/solution.py
@@ -78,12 +78,13 @@
     spc = spc.reshape(2, parts, cpd, a_loc * rep, n2_len).transpose(1, 2, 0, 3, 4)
     spc = spc.reshape(parts, cpd, 2 * a_loc * rep, n2_len)
     sig = signal.reshape(parts, cpd, slab // n2_len, n2_len)
-    buf = jnp.concatenate([spc, sig], axis=2)
+    buf = jnp.concatenate([sig, spc], axis=2)
     got = lax.all_to_all(buf, "seq", 0, 0, tiled=True)
     spec_rows = 2 * a_loc * rep
-    x = got[:, :, spec_rows:].transpose(1, 0, 2, 3).reshape(cpd, parts * slab)
+    sig_rows = slab // n2_len
+    x = got[:, :, :sig_rows].transpose(1, 0, 2, 3).reshape(cpd, parts * slab)
     half_rows = spec_rows // 2
-    s = [got[:, :, h * half_rows:(h + 1) * half_rows].astype(jnp.float32)
+    s = [got[:, :, sig_rows + h * half_rows:sig_rows + (h + 1) * half_rows].astype(jnp.float32)
          .transpose(1, 0, 2, 3).reshape(cpd, n1_len, n2_len) for h in range(2)]
     gain = lax.dynamic_slice_in_dim(skip_gain, seq_rank * cpd, cpd)
     out = local_conv(x, s, gain, n1_len, km)

time: 96.3 us -> 96.9 us (level)
  no operation moved by 1% of the time
where the time goes in v8:
time: 96.9 us; the launch traced here: 96.5 us
  waiting for transfers between devices  27.3 us (28%)
  blocking collectives  19.6 us (20%)
  local copies, waits for them, and re-layouts  17.4 us (18%)
  starting transfers between devices  15.2 us (16%)
  other arithmetic  8.73 us (9%)
  matrix products  8.03 us (8%)
    all_to_all x1, waiting for transfers between devices, per_device(): got = lax.all_to_all(buf, 'seq', 0, 0, tiled=True)  27.3 us
    all_to_all x1, blocking collectives, per_device(): back = lax.all_to_all(back, 'seq', 0, 0, tiled=True)  19.6 us
    all_to_all x1, starting transfers between devices, per_device(): got = lax.all_to_all(buf, 'seq', 0, 0, tiled=True)  15.2 us
    dot_general x3, matrix products, dot_hi(): jnp.einsum(form, left, right, precision=lax.Precision.HIGH, preferred_ele...  4.91 us
    sin x1, other arithmetic, local_conv(): tab_c, tab_s = lax.optimization_barrier((jnp.cos(angles), jnp.sin(angles)))  3.78 us
    unnamed x20, local copies, waits for them, and re-layouts  2.93 us
    slice x2, local copies, waits for them, and re-layouts, local_conv(): tc, ts = (tab_c[n1_len + n2_len:], tab_s[n1_len + n2_len:])  2.86 us
    another operation x2, local copies, waits for them, and re-layouts, local_conv(): w = jnp.stack([wc, ws])  2.69 us
  transfers between devices with their start and end apart: 1, of which 1 were waited for; matrix products, arithmetic and copies ran while one was open for 13% of the time, Pallas kernels for 0%

profile of v8, /device:TPU:14, one launch (start us, length us, event | category | flops | bytes accessed | tf_op | source)
XLA Modules:
  0.0 96.5 jit_solution(13122204581975783689)
XLA Ops:
  0.0 0.0 copy-start
  0.0 1.2 %copy-done = bf16[2,128,2,1024]{3,2,1,0:T(2,128)(2,1)S(1)} copy-done((bf16[2,128,2,1024]{3,2,1,0:T(2,128)(2,1)S(1)}, bf16[2,128,2,1024]{3,2,1,0:T(2,128)(2,1)}, u32[]{:S(2)}) %copy-start) | copy-done | bytes 1048600
  1.2 1.3 %fusion.15 = bf16[2,128,2,1024]{1,3,2,0:T(8,128)(2,1)S(1)} fusion(s32[1024]{0:T(1024)S(1)} %fusion.70, bf16[2,128,2,1024]{3,2,1,0:T(2,128)(2,1)S(1)} %copy-done), kind=kOutput, calls=%fused_computation.19 | convolution fusion | flops 1075314688 | bytes 2101248 | tf_op jit(solution)/shard_map/rcab,bq->rcaq/dot_general | solution.py:76
  2.5 1.0 %copy.91 = bf16[2,128,2,1024]{3,2,1,0:T(2,128)(2,1)S(1)} copy(bf16[2,128,2,1024]{1,3,2,0:T(8,128)(2,1)S(1)} %fusion.15) | data formatting | bytes 2097152 | tf_op jit(solution)/shard_map/convert_element_type | solution.py:77
  3.5 0.0 copy-start.7
  3.5 0.4 reshape.438
  4.0 0.1 copy_bitcast_fusion
  4.1 0.4 copy-done.7
  4.5 0.2 reshape.437
  4.7 0.8 pad_maximum_fusion
  5.5 0.0 copy-start.8
  5.5 1.6 %copy.93 = bf16[32,4,20,256]{3,1,2,0:T(4,128)(2,1)} copy(bf16[32,4,20,256]{3,2,1,0:T(8,128)(2,1)S(1)} %pad_maximum_fusion) | data formatting | bytes 2621440 | tf_op jit(solution)/shard_map/concatenate | solution.py:81
  7.1 15.2 %all-to-all-start = ((bf16[32,4,20,256]{3,1,2,0:T(4,128)(2,1)}), bf16[32,4,20,256]{3,1,2,0:T(4,128)(2,1)S(1)}, u32[]{:S(2)}, u32[]{:S(2)}) async-start(bf16[32,4,20,256]{3,1,2,0:T(4,128)(2,1)} %copy.93), calls=%async_computation | async-start | bytes 2621440 | tf_op jit(solution)/shard_map/all_to_all | solution.py:82
  22.4 0.0 copy-done.8
  22.4 0.4 fusion.42
  22.8 3.8 %fusion.36 = (f32[768,256]{1,0:T(8,128)S(1)}, f32[768,256]{1,0:T(8,128)}) fusion(f32[256,256]{1,0:T(8,128)S(1)} %get-tuple-element.32, f32[256,256]{1,0:T(8,128)S(1)} %get-tuple-element.33, f32[256,256]{1,0:T(8,128)S(1)} %get-tuple-element.31), kind=kLoop, calls=%fused_computation.50 | loop fusion | flops 393216 | bytes 2359296 | tf_op jit(solution)/shard_map/sin | solution.py:33
  26.6 0.0 copy-start.9
  26.6 0.8 slice_bitcast_fusion.4
  27.4 1.1 %copy.100 = f32[256,256]{0,1:T(8,128)S(1)} copy(f32[256,256]{1,0:T(8,128)} %get-tuple-element.24) | data formatting | bytes 524288 | tf_op jit(solution)/shard_map/slice | solution.py:36
  28.5 1.9 %slice_bitcast_fusion.5 = (f32[1,256,256]{2,1,0:T(8,128)}, f32[256,256]{1,0:T(8,128)}) fusion(f32[768,256]{1,0:T(8,128)} %get-tuple-element.7), kind=kLoop, calls=%fused_computation.91 | loop fusion | bytes 1048576 | tf_op jit(solution)/shard_map/stack | solution.py:47
  30.4 1.8 %copy.99 = f32[256,256]{0,1:T(8,128)} copy(f32[256,256]{1,0:T(8,128)} %get-tuple-element.22) | data formatting | bytes 524288 | tf_op jit(solution)/shard_map/slice | solution.py:36
  32.1 0.0 copy-done.9
  32.1 0.1 dynamic_slice.3
  32.2 0.9 slice_bitcast_fusion.6
  33.1 0.7 fusion.62
  33.8 0.8 reduce-precision_convert_fusion
  34.6 27.3 %all-to-all-done = bf16[32,4,20,256]{3,1,2,0:T(4,128)(2,1)S(1)} async-done(((bf16[32,4,20,256]{3,1,2,0:T(4,128)(2,1)}), bf16[32,4,20,256]{3,1,2,0:T(4,128)(2,1)S(1)}, u32[]{:S(2)}, u32[]{:S(2)}) %all-to-all-start) | async-done | bytes 1310752 | tf_op jit(solution)/shard_map/all_to_all | solution.py:82
  61.8 0.1 slice.84
  61.9 0.9 convert_bitcast_fusion.2
  62.8 0.9 copy.95
  63.7 0.6 fusion.81
  64.3 0.2 convert_bitcast_fusion
  64.5 1.3 %copy.106 = f32[1,4,256,256]{2,3,1,0:T(8,128)} copy(f32[1,4,256,256]{3,2,1,0:T(8,128)S(1)} %get-tuple-element.35) | data formatting | bytes 2097152 | tf_op jit(solution)/shard_map/reshape | solution.py:88
  65.9 0.3 copy.108
  66.2 0.0 copy-start.2
  66.2 1.8 %convolution_bitcast_fusion.2 = f32[2,2,4,256,256]{3,4,1,0,2:T(8,128)S(1)} fusion(bf16[1,2,256,128]{3,2,1,0:T(8,128)(2,1)} %get-tuple-element.30, bf16[1,2,256,128]{3,2,1,0:T(8,128)(2,1)} %get-tuple-element.29, bf16[4,128,256,1,1]{2,0,1,4,3:T(4,128)(2,1)} %bitcast.161), kind=kOutput, calls=%fused_computation.5 | convolution fusion | flops 268959744 | bytes 4718592 | tf_op jit(solution)/shard_map/hzkn,cnm->hzckm/dot_general | solution.py:42
  68.0 0.0 copy-done.2
  68.1 0.0 copy-start.3
  68.1 0.0 copy-start.4
  68.1 0.3 multiply_add_fusion.2
  68.4 0.6 copy-done.3
  69.0 0.1 copy-done.4
  69.1 0.0 copy-start.1
  69.1 2.0 %convolution_bitcast_fusion.1 = f32[2,2,4,256,256]{3,4,2,0,1:T(8,128)S(1)} fusion(f32[1,4,256,256]{2,3,1,0:T(8,128)S(1)} %get-tuple-element.14, f32[1,4,256,256]{2,3,1,0:T(8,128)S(1)} %get-tuple-element.13, f32[1,256,256]{2,1,0:T(8,128)S(1)} %copy-done.3, f32[1,256,256]{2,1,0:T(8,128)S(1)} %copy-done.4), kind=kOutput, calls=%fused_computation.4 | convolution fusion | flops 1611268096 | bytes 6815744 | tf_op jit(solution)/shard_map/zckn,wnj->zwckj/dot_general | solution.py:10
  71.1 0.0 copy-done.1
  71.1 0.4 multiply_subtract_fusion.1
  71.5 1.9 %convolution_bitcast_fusion = f32[2,2,4,256,256]{3,4,2,1,0:T(8,128)S(1)} fusion(f32[1,4,256,256]{2,3,1,0:T(8,128)S(1)} %get-tuple-element.10, f32[1,4,256,256]{2,3,1,0:T(8,128)S(1)} %get-tuple-element.9, f32[1,256,256]{2,1,0:T(8,128)S(1)} %copy-done.3, f32[1,256,256]{2,1,0:T(8,128)S(1)} %copy-done.4), kind=kOutput, calls=%fused_computation.3 | convolution fusion | flops 1611268096 | bytes 6815744 | tf_op jit(solution)/shard_map/zckj,wjn->zwckn/dot_general | solution.py:10
  73.4 0.0 copy-start.6
  73.5 0.3 multiply_subtract_fusion
  73.8 0.6 copy-done.6
  74.4 0.0 copy-start.5
  74.4 1.0 %fusion.24 = f32[4,128,256]{1,2,0:T(8,128)S(1)} fusion(f32[1,4,256,256]{2,3,1,0:T(8,128)S(1)} %get-tuple-element.12, f32[1,4,256,256]{2,3,1,0:T(8,128)S(1)} %get-tuple-element.11, f32[1,256,128]{2,1,0:T(8,128)S(1)} %copy-done.6, f32[1,256,128]{2,1,0:T(8,128)S(1)} %get-tuple-element.17), kind=kOutput, calls=%fused_computation.22 | convolution fusion | flops 403374080 | bytes 2883584 | tf_op jit(solution)/shard_map/zkn,zckm->cnm/dot_general | solution.py:10
  75.4 0.2 copy.114
  75.6 0.1 mul.280
  75.7 0.0 copy-done.5
  75.8 0.1 fusion.50
  75.9 0.2 copy.116
  76.1 19.6 %all_to_all.10 = bf16[32,4,1024]{2,1,0:T(4,128)(2,1)S(1)} all-to-all(bf16[32,4,1024]{2,1,0:T(4,128)(2,1)S(1)} %copy.116), channel_id=1, replica_groups=mesh['seq'=32,'chan'=16] {'seq'}, dimensions={0} | all-to-all | bytes 524288 | tf_op jit(solution)/shard_map/all_to_all | solution.py:92
  95.7 0.8 reshape.444
  (3 shorter events, 0.1 us)
Async XLA Ops:
  0.0 1.2 %copy-start = (bf16[2,128,2,1024]{3,2,1,0:T(2,128)(2,1)S(1)}, bf16[2,128,2,1024]{3,2,1,0:T(2,128)(2,1)}, u32[]{:S(2)}) copy-start(bf16[2,128,2,1024]{3,2,1,0:T(2,128)(2,1)} %param.4) | copy-start | bytes 3145732
  3.5 1.0 copy-start.7
  5.5 16.9 %copy-start.8 = (s32[256]{0:T(256)S(1)}, s32[256]{0:T(256)}, u32[]{:S(2)}) copy-start(s32[256]{0:T(256)} %constant.91.clone.1) | copy-start | bytes 3076
  7.1 54.8 %all-to-all-start = ((bf16[32,4,20,256]{3,1,2,0:T(4,128)(2,1)}), bf16[32,4,20,256]{3,1,2,0:T(4,128)(2,1)S(1)}, u32[]{:S(2)}, u32[]{:S(2)}) async-start(bf16[32,4,20,256]{3,1,2,0:T(4,128)(2,1)} %copy.93), calls=%async_computation | async-start | bytes 2621440 | tf_op jit(solution)/shard_map/all_to_all | solution.py:82
  26.6 5.6 %copy-start.9 = (f32[128]{0:T(128)S(1)}, f32[128]{0:T(128)}, u32[]{:S(2)}) copy-start(f32[128]{0:T(128)} %param.5) | copy-start | bytes 1540
  66.2 1.8 %copy-start.2 = (f32[256,256]{0,1:T(8,128)S(1)}, f32[256,256]{0,1:T(8,128)}, u32[]{:S(2)}) copy-start(f32[256,256]{0,1:T(8,128)} %copy.99) | copy-start | bytes 786436
  68.1 1.0 copy-start.3
  68.1 1.0 %copy-start.4 = (f32[1,256,256]{2,1,0:T(8,128)S(1)}, f32[1,256,256]{2,1,0:T(8,128)}, u32[]{:S(2)}) copy-start(f32[1,256,256]{2,1,0:T(8,128)} %get-tuple-element.21) | copy-start | bytes 786436
  69.1 2.0 %copy-start.1 = (f32[1,4,256,256]{2,3,1,0:T(8,128)S(1)}, f32[1,4,256,256]{2,3,1,0:T(8,128)}, u32[]{:S(2)}) copy-start(f32[1,4,256,256]{2,3,1,0:T(8,128)} %copy.106) | copy-start | bytes 3145732
  73.4 0.9 copy-start.6
  74.4 1.4 %copy-start.5 = (f32[4,4,4,8,256]{4,3,2,1,0:T(8,128)S(1)}, f32[4,4,4,8,256]{4,3,2,1,0:T(8,128)}, u32[]{:S(2)}) copy-start(f32[4,4,4,8,256]{4,3,2,1,0:T(8,128)} %get-tuple-element.27) | copy-start | bytes 1572868

commit v9 on v6

--- a/solution.py
+++ b/solution.py
@@ -73,8 +73,8 @@
     seq_rank = lax.axis_index("seq")
     cols = jnp.arange(nb, dtype=jnp.int32)
     perm = cols[:, None] == (cols[None, :] % n2_len) * rep + cols[None, :] // n2_len
-    spc = jnp.einsum("rcab,bq->rcaq", spectrum, perm.astype(jnp.bfloat16),
-                     preferred_element_type=jnp.float32).astype(jnp.bfloat16)
+    spc = jnp.dot(spectrum.reshape(-1, nb), perm.astype(jnp.bfloat16),
+                  preferred_element_type=jnp.bfloat16)
     spc = spc.reshape(2, parts, cpd, a_loc * rep, n2_len).transpose(1, 2, 0, 3, 4)
     spc = spc.reshape(parts, cpd, 2 * a_loc * rep, n2_len)
     sig = signal.reshape(parts, cpd, slab // n2_len, n2_len)

time: 96.3 us -> 95.1 us (0.988)
  local copies, waits for them, and re-layouts: 17.4 us -> 12.1 us
  waiting for transfers between devices: 27.3 us -> 32.3 us
  other arithmetic: 8.12 us -> 7.11 us
    all_to_all x1, waiting for transfers between devices: 27.3 us -> 32.3 us  [per_device(): got = lax.all_to_all(buf, 'seq', 0, 0, tiled=True)]
    slice x2, local copies, waits for them, and re-layouts: 2.86 us -> 0.96 us  [local_conv(): tc, ts = (tab_c[n1_len + n2_len:], tab_s[n1_len + n2_len:])]
    reshape x0 -> x1, local copies, waits for them, and re-layouts: none -> 1.46 us  [per_device(): spectrum.reshape(-1, nb)]
    unnamed x20 -> x16, local copies, waits for them, and re-layouts: 2.93 us -> 1.48 us
    unnamed x0 -> x1, matrix products: none -> 1.3 us
    dot_general x1 -> x0, matrix products: 1.29 us -> none  [per_device(): jnp.einsum('rcab,bq->rcaq', spectrum, perm.astype(jnp.bfloat16), preferre...]
    another operation x2, local copies, waits for them, and re-layouts: 2.69 us -> 1.47 us  [local_conv(): w = jnp.stack([wc, ws])]
    sin x1, other arithmetic: 3.78 us -> 2.75 us  [local_conv(): tab_c, tab_s = lax.optimization_barrier((jnp.cos(angles), jnp.sin(angles)))]
  transfers between devices with their start and end apart: 1 -> 1, of which waited for: 1 -> 1; matrix products, arithmetic and copies ran while one was open for 13% -> 8% of each run, Pallas kernels for 0% -> 0%
where the time goes in v9:
time: 95.1 us; the launch traced here: 94.7 us
  waiting for transfers between devices  32.3 us (34%)
  blocking collectives  19.6 us (21%)
  starting transfers between devices  15.2 us (16%)
  local copies, waits for them, and re-layouts  12.1 us (13%)
  matrix products  8.04 us (8%)
  other arithmetic  7.11 us (7%)
    all_to_all x1, waiting for transfers between devices, per_device(): got = lax.all_to_all(buf, 'seq', 0, 0, tiled=True)  32.3 us
    all_to_all x1, blocking collectives, per_device(): back = lax.all_to_all(back, 'seq', 0, 0, tiled=True)  19.6 us
    all_to_all x1, starting transfers between devices, per_device(): got = lax.all_to_all(buf, 'seq', 0, 0, tiled=True)  15.2 us
    dot_general x3, matrix products, dot_hi(): jnp.einsum(form, left, right, precision=lax.Precision.HIGH, preferred_ele...  4.91 us
    sin x1, other arithmetic, local_conv(): tab_c, tab_s = lax.optimization_barrier((jnp.cos(angles), jnp.sin(angles)))  2.75 us
  transfers between devices with their start and end apart: 1, of which 1 were waited for; matrix products, arithmetic and copies ran while one was open for 8% of the time, Pallas kernels for 0%

profile of v9, /device:TPU:14, one launch (start us, length us, event | category | flops | bytes accessed | tf_op | source)
XLA Modules:
  0.0 94.7 jit_solution(5680885961691155052)
XLA Ops:
  0.0 1.5 %reshape.440 = bf16[512,1024]{1,0:T(8,128)(2,1)S(1)} reshape(bf16[2,128,2,1024]{3,2,1,0:T(2,128)(2,1)} %param.4) | data formatting | bytes 2097152 | tf_op jit(solution)/shard_map/reshape | solution.py:76
  1.5 1.3 %fusion.15 = bf16[512,1024]{0,1:T(8,128)(2,1)S(1)} fusion(bf16[512,1024]{1,0:T(8,128)(2,1)S(1)} %reshape.440, s32[1024]{0:T(1024)S(1)} %fusion.69), kind=kOutput, calls=%fused_computation.19 | convolution fusion | flops 1076363264 | bytes 2101248
  2.8 0.5 copy.89
  3.3 0.0 copy-start.5
  3.3 0.7 reshape.441
  4.0 0.1 copy_bitcast_fusion
  4.1 0.2 copy-done.5
  4.3 0.2 reshape.443
  4.5 0.2 pad_maximum_fusion
  4.7 0.0 copy-start.6
  4.7 1.6 %copy.91 = bf16[32,4,20,256]{3,1,2,0:T(4,128)(2,1)} copy(bf16[32,4,20,256]{3,2,1,0:T(8,128)(2,1)S(1)} %pad_maximum_fusion) | data formatting | bytes 2621440 | tf_op jit(solution)/shard_map/concatenate | solution.py:81
  6.3 15.2 %all-to-all-start = ((bf16[32,4,20,256]{3,1,2,0:T(4,128)(2,1)}), bf16[32,4,20,256]{3,1,2,0:T(4,128)(2,1)S(1)}, u32[]{:S(2)}, u32[]{:S(2)}) async-start(bf16[32,4,20,256]{3,1,2,0:T(4,128)(2,1)} %copy.91), calls=%async_computation | async-start | bytes 2621440 | tf_op jit(solution)/shard_map/all_to_all | solution.py:82
  21.6 0.0 copy-done.6
  21.6 0.4 fusion.41
  22.0 2.8 %fusion.35 = (f32[768,256]{1,0:T(8,128)S(1)}, f32[768,256]{1,0:T(8,128)S(1)}) fusion(f32[256,256]{1,0:T(8,128)S(1)} %get-tuple-element.32, f32[256,256]{1,0:T(8,128)S(1)} %get-tuple-element.33, f32[256,256]{1,0:T(8,128)S(1)} %get-tuple-element.31), kind=kLoop, calls=%fused_computation.49 | loop fusion | flops 393216 | bytes 2359296 | tf_op jit(solution)/shard_map/sin | solution.py:33
  24.8 0.0 copy-start.7
  24.8 0.7 slice_bitcast_fusion.5
  25.5 0.1 copy.97
  25.6 0.7 slice_bitcast_fusion.4
  26.4 0.8 copy.98
  27.2 0.0 copy-done.7
  27.2 0.1 dynamic_slice.3
  27.3 0.7 fusion.61
  28.0 0.8 reduce-precision_convert_fusion
  28.7 32.3 %all-to-all-done = bf16[32,4,20,256]{3,1,2,0:T(4,128)(2,1)S(1)} async-done(((bf16[32,4,20,256]{3,1,2,0:T(4,128)(2,1)}), bf16[32,4,20,256]{3,1,2,0:T(4,128)(2,1)S(1)}, u32[]{:S(2)}, u32[]{:S(2)}) %all-to-all-start) | async-done | bytes 1310752 | tf_op jit(solution)/shard_map/all_to_all | solution.py:82
  61.1 0.1 slice.84
  61.2 0.9 convert_bitcast_fusion.2
  62.1 0.9 copy.93
  63.0 0.6 fusion.80
  63.6 0.2 convert_bitcast_fusion
  63.8 0.3 copy.104
  64.1 0.3 copy.106
  64.4 0.0 copy-start
  64.5 1.8 %convolution_bitcast_fusion.2 = f32[2,2,4,256,256]{3,4,1,0,2:T(8,128)S(1)} fusion(bf16[1,2,256,128]{3,2,1,0:T(8,128)(2,1)} %get-tuple-element.30, bf16[1,2,256,128]{3,2,1,0:T(8,128)(2,1)} %get-tuple-element.29, bf16[4,128,256,1,1]{2,0,1,4,3:T(4,128)(2,1)} %bitcast.153), kind=kOutput, calls=%fused_computation.4 | convolution fusion | flops 268959744 | bytes 4718592 | tf_op jit(solution)/shard_map/hzkn,cnm->hzckm/dot_general | solution.py:42
  66.3 0.0 copy-done
  66.3 0.0 copy-start.1
  66.3 0.0 copy-start.2
  66.3 0.3 multiply_add_fusion.2
  66.6 0.6 copy-done.1
  67.2 0.1 copy-done.2
  67.3 1.9 %convolution_bitcast_fusion.1 = f32[2,2,4,256,256]{3,4,2,0,1:T(8,128)S(1)} fusion(f32[1,4,256,256]{2,3,1,0:T(8,128)S(1)} %get-tuple-element.14, f32[1,4,256,256]{2,3,1,0:T(8,128)S(1)} %get-tuple-element.13, f32[1,256,256]{2,1,0:T(8,128)S(1)} %copy-done.2, f32[1,256,256]{2,1,0:T(8,128)S(1)} %copy-done.1), kind=kOutput, calls=%fused_computation.3 | convolution fusion | flops 1611268096 | bytes 6815744 | tf_op jit(solution)/shard_map/zckn,wnj->zwckj/dot_general | solution.py:10
  69.2 0.4 multiply_subtract_fusion.1
  69.7 2.0 %convolution_bitcast_fusion = f32[2,2,4,256,256]{3,4,2,1,0:T(8,128)S(1)} fusion(f32[1,4,256,256]{2,3,1,0:T(8,128)S(1)} %get-tuple-element.10, f32[1,4,256,256]{2,3,1,0:T(8,128)S(1)} %get-tuple-element.9, f32[1,256,256]{2,1,0:T(8,128)S(1)} %copy-done.2, f32[1,256,256]{2,1,0:T(8,128)S(1)} %copy-done.1), kind=kOutput, calls=%fused_computation.2 | convolution fusion | flops 1611268096 | bytes 6815744 | tf_op jit(solution)/shard_map/zckj,wjn->zwckn/dot_general | solution.py:10
  71.7 0.0 copy-start.4
  71.7 0.3 multiply_subtract_fusion
  72.0 0.6 copy-done.4
  72.6 0.0 copy-start.3
  72.6 1.0 %fusion.24 = f32[4,128,256]{1,2,0:T(8,128)S(1)} fusion(f32[1,4,256,256]{2,3,1,0:T(8,128)S(1)} %get-tuple-element.12, f32[1,4,256,256]{2,3,1,0:T(8,128)S(1)} %get-tuple-element.11, f32[1,256,128]{2,1,0:T(8,128)S(1)} %copy-done.4, f32[1,256,128]{2,1,0:T(8,128)S(1)} %get-tuple-element.17), kind=kOutput, calls=%fused_computation.22 | convolution fusion | flops 403374080 | bytes 2883584 | tf_op jit(solution)/shard_map/zkn,zckm->cnm/dot_general | solution.py:10
  73.6 0.2 copy.112
  73.8 0.1 mul.280
  73.9 0.0 copy-done.3
  74.0 0.1 fusion.49
  74.1 0.2 copy.114
  74.4 19.6 %all_to_all.10 = bf16[32,4,1024]{2,1,0:T(4,128)(2,1)S(1)} all-to-all(bf16[32,4,1024]{2,1,0:T(4,128)(2,1)S(1)} %copy.114), channel_id=1, replica_groups=mesh['seq'=32,'chan'=16] {'seq'}, dimensions={0} | all-to-all | bytes 524288 | tf_op jit(solution)/shard_map/all_to_all | solution.py:91
  94.0 0.8 reshape.448
  (4 shorter events, 0.1 us)
Async XLA Ops:
  3.3 1.0 %copy-start.5 = (bf16[128,1024]{1,0:T(8,128)(2,1)S(1)}, bf16[128,1024]{1,0:T(8,128)(2,1)}, u32[]{:S(2)}) copy-start(bf16[128,1024]{1,0:T(8,128)(2,1)} %param.3) | copy-start | bytes 786436
  4.7 16.9 %copy-start.6 = (s32[256]{0:T(256)S(1)}, s32[256]{0:T(256)}, u32[]{:S(2)}) copy-start(s32[256]{0:T(256)} %constant.91.clone.1) | copy-start | bytes 3076
  6.3 54.8 %all-to-all-start = ((bf16[32,4,20,256]{3,1,2,0:T(4,128)(2,1)}), bf16[32,4,20,256]{3,1,2,0:T(4,128)(2,1)S(1)}, u32[]{:S(2)}, u32[]{:S(2)}) async-start(bf16[32,4,20,256]{3,1,2,0:T(4,128)(2,1)} %copy.91), calls=%async_computation | async-start | bytes 2621440 | tf_op jit(solution)/shard_map/all_to_all | solution.py:82
  24.8 2.5 %copy-start.7 = (f32[128]{0:T(128)S(1)}, f32[128]{0:T(128)}, u32[]{:S(2)}) copy-start(f32[128]{0:T(128)} %param.5) | copy-start | bytes 1540
  64.4 1.8 %copy-start = (f32[256,256]{0,1:T(8,128)S(1)}, f32[256,256]{0,1:T(8,128)}, u32[]{:S(2)}) copy-start(f32[256,256]{0,1:T(8,128)} %copy.98) | copy-start | bytes 786436
  66.3 1.0 %copy-start.1 = (f32[1,256,256]{2,1,0:T(8,128)S(1)}, f32[1,256,256]{2,1,0:T(8,128)}, u32[]{:S(2)}) copy-start(f32[1,256,256]{2,1,0:T(8,128)} %get-tuple-element.21) | copy-start | bytes 786436
  66.3 1.0 %copy-start.2 = (f32[1,256,256]{2,1,0:T(8,128)S(1)}, f32[1,256,256]{2,1,0:T(8,128)}, u32[]{:S(2)}) copy-start(f32[1,256,256]{2,1,0:T(8,128)} %get-tuple-element.23) | copy-start | bytes 786436
  71.7 0.9 copy-start.4
  72.6 1.4 %copy-start.3 = (f32[4,4,4,8,256]{4,3,2,1,0:T(8,128)S(1)}, f32[4,4,4,8,256]{4,3,2,1,0:T(8,128)}, u32[]{:S(2)}) copy-start(f32[4,4,4,8,256]{4,3,2,1,0:T(8,128)} %get-tuple-element.27) | copy-start | bytes 1572868

commit v10 on v9

--- a/solution.py
+++ b/solution.py
@@ -79,7 +79,9 @@
     spc = spc.reshape(parts, cpd, 2 * a_loc * rep, n2_len)
     sig = signal.reshape(parts, cpd, slab // n2_len, n2_len)
     buf = jnp.concatenate([spc, sig], axis=2)
-    got = lax.all_to_all(buf, "seq", 0, 0, tiled=True)
+    rows_per = buf.shape[2]
+    buf = buf.reshape(parts, cpd * rows_per, n2_len)
+    got = lax.all_to_all(buf, "seq", 0, 0, tiled=True).reshape(parts, cpd, rows_per, n2_len)
     spec_rows = 2 * a_loc * rep
     x = got[:, :, spec_rows:].transpose(1, 0, 2, 3).reshape(cpd, parts * slab)
     half_rows = spec_rows // 2

time: 95.1 us -> 97 us (1.020)
  local copies, waits for them, and re-layouts: 12.1 us -> 14 us
    reshape x0 -> x1, local copies, waits for them, and re-layouts: none -> 1.81 us  [per_device(): buf = buf.reshape(parts, cpd * rows_per, n2_len)]
    reshape x2 -> x3, local copies, waits for them, and re-layouts: 0.66 us -> 1.86 us  [per_device(): s = [got[:, :, h * half_rows:(h + 1) * half_rows].astype(jnp.float32).tra...]
where the time goes in v10:
time: 97 us; the launch traced here: 96.6 us
  waiting for transfers between devices  32.3 us (33%)
  blocking collectives  19.6 us (20%)
  starting transfers between devices  15.1 us (16%)
  local copies, waits for them, and re-layouts  14 us (14%)
  matrix products  8.04 us (8%)
  other arithmetic  7.3 us (8%)
    all_to_all x1, waiting for transfers between devices, per_device(): lax.all_to_all(buf, 'seq', 0, 0, tiled=True)  32.3 us
    all_to_all x1, blocking collectives, per_device(): back = lax.all_to_all(back, 'seq', 0, 0, tiled=True)  19.6 us
    all_to_all x1, starting transfers between devices, per_device(): lax.all_to_all(buf, 'seq', 0, 0, tiled=True)  15.1 us
    dot_general x3, matrix products, dot_hi(): jnp.einsum(form, left, right, precision=lax.Precision.HIGH, preferred_ele...  4.91 us
    sin x1, other arithmetic, local_conv(): tab_c, tab_s = lax.optimization_barrier((jnp.cos(angles), jnp.sin(angles)))  2.93 us
  transfers between devices with their start and end apart: 1, of which 1 were waited for; matrix products, arithmetic and copies ran while one was open for 8% of the time, Pallas kernels for 0%

profile of v10, /device:TPU:14, one launch (start us, length us, event | category | flops | bytes accessed | tf_op | source)
XLA Modules:
  0.0 96.6 jit_solution(14376891949178961892)
XLA Ops:
  0.0 1.5 %reshape.446 = bf16[512,1024]{1,0:T(8,128)(2,1)S(1)} reshape(bf16[2,128,2,1024]{3,2,1,0:T(2,128)(2,1)} %param.4) | data formatting | bytes 2097152 | tf_op jit(solution)/shard_map/reshape | solution.py:76
  1.5 1.3 %fusion.15 = bf16[512,1024]{0,1:T(8,128)(2,1)S(1)} fusion(bf16[512,1024]{1,0:T(8,128)(2,1)S(1)} %reshape.446, s32[1024]{0:T(1024)S(1)} %fusion.69), kind=kOutput, calls=%fused_computation.19 | convolution fusion | flops 1076363264 | bytes 2101248
  2.8 0.5 copy.66
  3.3 0.0 copy-start.5
  3.3 0.7 reshape.447
  4.0 0.1 copy_bitcast_fusion.2
  4.1 0.2 copy-done.5
  4.3 0.2 reshape.449
  4.5 0.2 pad_maximum_fusion
  4.7 0.7 copy.68
  5.4 0.0 copy-start.6
  5.4 1.8 %copy.69 = bf16[32,80,256]{2,1,0:T(8,128)(2,1)} copy(bf16[32,80,256]{2,0,1:T(8,128)(2,1)S(1)} %bitcast.156) | data formatting | bytes 2621440 | tf_op jit(solution)/shard_map/reshape | solution.py:83
  7.2 15.1 %all-to-all-start = ((bf16[32,80,256]{2,1,0:T(8,128)(2,1)}), bf16[32,80,256]{2,1,0:T(8,128)(2,1)S(1)}, u32[]{:S(2)}, u32[]{:S(2)}) async-start(bf16[32,80,256]{2,1,0:T(8,128)(2,1)} %copy.69), calls=%async_computation | async-start | bytes 2621440 | tf_op jit(solution)/shard_map/all_to_all | solution.py:84
  22.3 0.0 copy-done.6
  22.3 0.4 fusion.41
  22.8 2.9 %fusion.35 = (f32[768,256]{1,0:T(8,128)S(1)}, f32[768,256]{1,0:T(8,128)S(1)}) fusion(f32[256,256]{1,0:T(8,128)S(1)} %get-tuple-element.32, f32[256,256]{1,0:T(8,128)S(1)} %get-tuple-element.33, f32[256,256]{1,0:T(8,128)S(1)} %get-tuple-element.31), kind=kLoop, calls=%fused_computation.51 | loop fusion | flops 393216 | bytes 2359296 | tf_op jit(solution)/shard_map/sin | solution.py:33
  25.7 0.0 copy-start.7
  25.7 0.7 slice_bitcast_fusion.6
  26.5 0.1 copy.75
  26.6 0.7 slice_bitcast_fusion.5
  27.3 0.8 copy.76
  28.2 0.0 copy-done.7
  28.2 0.1 dynamic_slice.3
  28.3 0.7 fusion.61
  28.9 0.8 reduce-precision_convert_fusion
  29.7 32.3 %all-to-all-done = bf16[32,80,256]{2,1,0:T(8,128)(2,1)S(1)} async-done(((bf16[32,80,256]{2,1,0:T(8,128)(2,1)}), bf16[32,80,256]{2,1,0:T(8,128)(2,1)S(1)}, u32[]{:S(2)}, u32[]{:S(2)}) %all-to-all-start) | async-done | bytes 1310752 | tf_op jit(solution)/shard_map/all_to_all | solution.py:84
  62.0 0.4 copy.70
  62.5 0.9 convert_bitcast_fusion.2
  63.3 0.3 convert_bitcast_fusion
  63.6 0.9 copy.71
  64.5 1.2 %copy_bitcast_fusion = (f32[1,4,256,256]{3,2,1,0:T(8,128)S(1)}, f32[1,4,256,256]{3,2,1,0:T(8,128)S(1)}) fusion(f32[4,32,8,256]{3,1,2,0:T(8,128)S(1)} %get-tuple-element.17, f32[4,32,8,256]{3,1,2,0:T(8,128)S(1)} %get-tuple-element.18), kind=kLoop, calls=%fused_computation.39 | loop fusion | bytes 4194304 | tf_op jit(solution)/shard_map/reshape | solution.py:89
  65.7 0.3 copy.82
  66.0 0.3 copy.84
  66.4 0.0 copy-start
  66.4 1.8 %convolution_bitcast_fusion.2 = f32[2,2,4,256,256]{3,4,1,0,2:T(8,128)S(1)} fusion(bf16[1,2,256,128]{3,2,1,0:T(8,128)(2,1)} %get-tuple-element.30, bf16[1,2,256,128]{3,2,1,0:T(8,128)(2,1)} %get-tuple-element.29, bf16[4,128,256,1,1]{2,0,1,4,3:T(4,128)(2,1)} %bitcast.158), kind=kOutput, calls=%fused_computation.4 | convolution fusion | flops 268959744 | bytes 4718592 | tf_op jit(solution)/shard_map/hzkn,cnm->hzckm/dot_general | solution.py:42
  68.2 0.0 copy-done
  68.2 0.0 copy-start.1
  68.2 0.0 copy-start.2
  68.2 0.3 multiply_add_fusion.2
  68.6 0.6 copy-done.1
  69.2 0.1 copy-done.2
  69.2 2.0 %convolution_bitcast_fusion.1 = f32[2,2,4,256,256]{3,4,2,0,1:T(8,128)S(1)} fusion(f32[1,4,256,256]{2,3,1,0:T(8,128)S(1)} %get-tuple-element.14, f32[1,4,256,256]{2,3,1,0:T(8,128)S(1)} %get-tuple-element.13, f32[1,256,256]{2,1,0:T(8,128)S(1)} %copy-done.2, f32[1,256,256]{2,1,0:T(8,128)S(1)} %copy-done.1), kind=kOutput, calls=%fused_computation.3 | convolution fusion | flops 1611268096 | bytes 6815744 | tf_op jit(solution)/shard_map/zckn,wnj->zwckj/dot_general | solution.py:10
  71.3 0.4 multiply_subtract_fusion.1
  71.7 1.9 %convolution_bitcast_fusion = f32[2,2,4,256,256]{3,4,2,1,0:T(8,128)S(1)} fusion(f32[1,4,256,256]{2,3,1,0:T(8,128)S(1)} %get-tuple-element.10, f32[1,4,256,256]{2,3,1,0:T(8,128)S(1)} %get-tuple-element.9, f32[1,256,256]{2,1,0:T(8,128)S(1)} %copy-done.2, f32[1,256,256]{2,1,0:T(8,128)S(1)} %copy-done.1), kind=kOutput, calls=%fused_computation.2 | convolution fusion | flops 1611268096 | bytes 6815744 | tf_op jit(solution)/shard_map/zckj,wjn->zwckn/dot_general | solution.py:10
  73.6 0.0 copy-start.4
  73.6 0.3 multiply_subtract_fusion
  73.9 0.6 copy-done.4
  74.5 0.0 copy-start.3
  74.5 1.0 %fusion.24 = f32[4,128,256]{1,2,0:T(8,128)S(1)} fusion(f32[1,4,256,256]{2,3,1,0:T(8,128)S(1)} %get-tuple-element.12, f32[1,4,256,256]{2,3,1,0:T(8,128)S(1)} %get-tuple-element.11, f32[1,256,128]{2,1,0:T(8,128)S(1)} %copy-done.4, f32[1,256,128]{2,1,0:T(8,128)S(1)} %get-tuple-element.19), kind=kOutput, calls=%fused_computation.22 | convolution fusion | flops 403374080 | bytes 2883584 | tf_op jit(solution)/shard_map/zkn,zckm->cnm/dot_general | solution.py:10
  75.5 0.2 copy.90
  75.7 0.1 mul.280
  75.9 0.0 copy-done.3
  75.9 0.1 fusion.49
  76.1 0.2 copy.92
  76.3 19.6 %all_to_all.10 = bf16[32,4,1024]{2,1,0:T(4,128)(2,1)S(1)} all-to-all(bf16[32,4,1024]{2,1,0:T(4,128)(2,1)S(1)} %copy.92), channel_id=1, replica_groups=mesh['seq'=32,'chan'=16] {'seq'}, dimensions={0} | all-to-all | bytes 524288 | tf_op jit(solution)/shard_map/all_to_all | solution.py:93
  95.9 0.8 reshape.456
  (4 shorter events, 0.1 us)
Async XLA Ops:
  3.3 1.0 copy-start.5
  5.4 16.9 %copy-start.6 = (s32[256]{0:T(256)S(1)}, s32[256]{0:T(256)}, u32[]{:S(2)}) copy-start(s32[256]{0:T(256)} %constant.91.clone.1) | copy-start | bytes 3076
  7.2 54.8 %all-to-all-start = ((bf16[32,80,256]{2,1,0:T(8,128)(2,1)}), bf16[32,80,256]{2,1,0:T(8,128)(2,1)S(1)}, u32[]{:S(2)}, u32[]{:S(2)}) async-start(bf16[32,80,256]{2,1,0:T(8,128)(2,1)} %copy.69), calls=%async_computation | async-start | bytes 2621440 | tf_op jit(solution)/shard_map/all_to_all | solution.py:84
  25.7 2.5 %copy-start.7 = (f32[128]{0:T(128)S(1)}, f32[128]{0:T(128)}, u32[]{:S(2)}) copy-start(f32[128]{0:T(128)} %param.5) | copy-start | bytes 1540
  66.4 1.8 %copy-start = (f32[256,256]{0,1:T(8,128)S(1)}, f32[256,256]{0,1:T(8,128)}, u32[]{:S(2)}) copy-start(f32[256,256]{0,1:T(8,128)} %copy.76) | copy-start | bytes 786436
  68.2 1.0 copy-start.1
  68.2 1.0 %copy-start.2 = (f32[1,256,256]{2,1,0:T(8,128)S(1)}, f32[1,256,256]{2,1,0:T(8,128)}, u32[]{:S(2)}) copy-start(f32[1,256,256]{2,1,0:T(8,128)} %get-tuple-element.25) | copy-start | bytes 786436
  73.6 0.9 copy-start.4
  74.5 1.4 %copy-start.3 = (f32[4,4,4,8,256]{4,3,2,1,0:T(8,128)S(1)}, f32[4,4,4,8,256]{4,3,2,1,0:T(8,128)}, u32[]{:S(2)}) copy-start(f32[4,4,4,8,256]{4,3,2,1,0:T(8,128)} %get-tuple-element.15) | copy-start | bytes 1572868
